TPU v7x, 128 devices: a whole 4x4x4 slice. The times are simulated.
128 devices in a mesh: ctx: 16 (over x, y_lo, core), tp: 8 (over y_hi, z).
Axes of the slice: x: 4, y: 4 (y_hi: 2, y_lo: 2; y = y_hi * 2 + y_lo), z: 4, core: 2. Of those that a mesh axis runs over, the one named last changes fastest.
Arguments:
- ctx_queries: bfloat16 [16384, 8192], P('ctx', 'tp'), may hold values from -70 to 70
- context_key_rows: bfloat16 [16384, 1024], P('ctx', 'tp'), may hold values from -4 to 4
- context_value_rows: bfloat16 [16384, 1024], P('ctx', 'tp'), may hold values from -6 to 6
- resp_queries: bfloat16 [512, 8192], P('ctx', 'tp'), may hold values from -70 to 70
- resp_keys: bfloat16 [512, 1024], P('ctx', 'tp'), may hold values from -4 to 4
- response_value_rows: bfloat16 [512, 1024], P('ctx', 'tp'), may hold values from -6 to 6
- split_index: int32 [1], replicated, may hold values from 64 to 448
- out_weight: bfloat16 [8192, 8192], P('tp'), may hold values from -0.0625 to 0.0625
Outputs:
- ctx_out: float32 [16384, 8192], P('ctx', 'tp')
- resp_out: float32 [512, 8192], P('ctx', 'tp')
All inputs are finite; a program needn't handle non-finite values.
Results may differ from a plain program's by a relative error of at most 0.005.
Values may be sent and summed in bfloat16 or wider, within the bound.
No kernel may reach another device: no remote copies, remote signals or barrier semaphores. Data moves between devices by JAX's collectives and lax.ppermute only.
A program may use at most 192 MiB of HBM per device.

v0:
```python
import jax
import jax.numpy as jnp
from jax import lax
from jax.sharding import PartitionSpec as P

HEAD_WIDTH = 128


NEGATIVE = -1e30


def spread_2(block, axis, source):
    block = jnp.where(lax.axis_index(axis) == source, block, jnp.zeros_like(block))
    return lax.psum(block, axis)


def joined(value, axis, join):
    pieces = jax.tree.map(lambda part: lax.all_gather(part, axis), value)
    head = jax.tree.map(lambda part: part[0], pieces)
    tail = jax.tree.map(lambda part: part[1:], pieces)
    so_far, _ = lax.scan(lambda so_far, piece: (join(so_far, piece), None), head, tail)
    return so_far


def partial_softmax(queries, key_rows, value_rows, visible, head_size):
    query_count = queries.shape[0]
    kv_heads = key_rows.shape[1] // head_size
    query_heads = queries.shape[1] // head_size
    group_size = query_heads // kv_heads
    score_scale = head_size ** (-0.5)
    stacked_queries = queries.reshape(query_count, query_heads, head_size).transpose(1, 0, 2)
    stacked_keys = key_rows.reshape(-1, kv_heads, head_size).transpose(1, 0, 2)
    stacked_values = value_rows.reshape(-1, kv_heads, head_size).transpose(1, 0, 2)

    def one_head(inputs):
        head_query, head_index = inputs
        head_keys = lax.dynamic_index_in_dim(
            stacked_keys, head_index // group_size, 0, keepdims=False
        )
        head_values = lax.dynamic_index_in_dim(
            stacked_values, head_index // group_size, 0, keepdims=False
        )
        scores = jnp.dot(head_query, head_keys.T, preferred_element_type=jnp.float32) * score_scale
        scores = jnp.where(visible, scores, NEGATIVE)
        row_max = jnp.max(scores, axis=1)
        weights = jnp.where(visible, jnp.exp(scores - row_max[:, None]), 0.0)
        row_sum = jnp.sum(weights, axis=1)
        numerator = jnp.dot(
            weights.astype(jnp.bfloat16), head_values, preferred_element_type=jnp.float32
        )
        return (row_max, row_sum, numerator)

    maxima, totals, numerator = lax.map(
        one_head, (stacked_queries, jnp.arange(query_heads, dtype=jnp.int32))
    )
    return (
        maxima.T,
        totals.T,
        numerator.transpose(1, 0, 2).reshape(query_count, query_heads * head_size),
    )


def spread(factor, width):
    return jnp.repeat(factor, width // factor.shape[1], axis=1)


def combine(earlier, later):
    joined_max = jnp.maximum(earlier[0], later[0])
    first_factor = jnp.exp(earlier[0] - joined_max)
    second_factor = jnp.exp(later[0] - joined_max)
    width = earlier[2].shape[1]
    totals = earlier[1] * first_factor + later[1] * second_factor
    numerator = earlier[2] * spread(first_factor, width) + later[2] * spread(second_factor, width)
    return (joined_max, totals, numerator)


def finish(maxima, totals, numerator):
    return numerator / spread(totals, numerator.shape[1])


def empty_state(row_count, query_heads, head_size):
    return (
        jnp.full((row_count, query_heads), NEGATIVE, jnp.float32),
        jnp.zeros((row_count, query_heads), jnp.float32),
        jnp.zeros((row_count, query_heads * head_size), jnp.float32),
    )


def on_device(
    ctx_queries,
    context_key_rows,
    context_value_rows,
    resp_queries,
    resp_keys,
    response_value_rows,
    split_index,
    out_weight,
):
    head_size = HEAD_WIDTH
    device = lax.axis_index("ctx")
    block_len = context_key_rows.shape[0]
    anchor = spread_2(jnp.stack([context_key_rows, context_value_rows]), "ctx", 0)
    joined_keys = jnp.concatenate([anchor[0], context_key_rows], axis=0)
    joined_values = jnp.concatenate([anchor[1], context_value_rows], axis=0)
    positions = jnp.arange(block_len, dtype=jnp.int32)
    own_visible = positions[None, :] <= positions[:, None]
    anchor_visible = jnp.broadcast_to(device > 0, (block_len, block_len))
    visible = jnp.concatenate([anchor_visible, own_visible], axis=1)
    ctx_out = finish(*partial_softmax(ctx_queries, joined_keys, joined_values, visible, head_size))
    resp_dev = resp_queries.shape[0]
    query_heads = resp_queries.shape[1] // head_size
    resp_total = resp_dev * lax.axis_size("ctx")
    own_start = device * resp_dev
    all_queries = lax.all_gather(resp_queries, "ctx", axis=0, tiled=True)
    seen_keys = jnp.ones((resp_total, block_len), dtype=bool)
    local_part = partial_softmax(
        all_queries, context_key_rows, context_value_rows, seen_keys, head_size
    )
    merged = joined((local_part[0], local_part[1], local_part[2]), "ctx", combine)
    context_part = tuple(
        (lax.dynamic_slice_in_dim(member, own_start, resp_dev, 0) for member in merged)
    )
    own_rows = own_start + jnp.arange(resp_dev, dtype=jnp.int32)
    boundary = split_index[0]
    portion = (
        lax.all_gather(resp_keys, "ctx", axis=0, tiled=True),
        lax.all_gather(response_value_rows, "ctx", axis=0, tiled=True),
    )
    key_pos = jnp.arange(portion[0].shape[0], dtype=jnp.int32)
    seen_rows = (key_pos[None, :] <= own_rows[:, None]) & (
        (key_pos[None, :] < boundary) == (own_rows[:, None] < boundary)
    )
    reply_part = combine(
        empty_state(resp_dev, query_heads, head_size),
        partial_softmax(resp_queries, portion[0], portion[1], seen_rows, head_size),
    )
    attended = finish(*combine(context_part, reply_part)).astype(jnp.bfloat16)
    projected = jnp.dot(attended, out_weight, preferred_element_type=jnp.float32)
    resp_out = lax.psum_scatter(projected, "tp", scatter_dimension=1, tiled=True)
    return (ctx_out, resp_out)


def solution(mesh):
    placed = (
        P("ctx", "tp"),
        P("ctx", "tp"),
        P("ctx", "tp"),
        P("ctx", "tp"),
        P("ctx", "tp"),
        P("ctx", "tp"),
        P(),
        P("tp", None),
    )
    return jax.shard_map(
        on_device,
        mesh=mesh,
        in_specs=placed,
        out_specs=(P("ctx", "tp"), P("ctx", "tp")),
        check_vma=False,
    )
```

profile of v0, /device:TPU:22, one launch (start us, length us, event | category | flops | bytes accessed | tf_op | source)
XLA Modules:
  0.0 596.0 jit_solution(18218528722244312762)
XLA Ops:
  10.0 32.9 %all-gather.5.cloned.1.call-done = bf16[512,1024]{1,0:T(8,128)(2,1)} async-done(((bf16[32,1024]{1,0:T(8,128)(2,1)}), bf16[512,1024]{1,0:T(8,128)(2,1)}) %all-gather.5.cloned.1.call-update) | async-done | bytes 1048592 | tf_op jit(solution)/shard_map/all_gather | solution.py:114
  44.3 19.7 %while.59 = (s32[]{:T(128)}, f32[8,512]{1,0:T(8,128)S(1)}, f32[8,512]{1,0:T(8,128)S(1)}, f32[8,512,128]{2,1,0:T(8,128)}, bf16[8,512,128]{1,2,0:T(8,128)(2,1)S(1)...) while((s32[]{:T(128)}, f32[8,512]{1,0:T(8,128)S(1)}, ...), condition=%wide.region_8.9_spmd, body=%wide.region_5.8_spmd.sunk | while | flops 272628736 | bytes 7225961 | solution.py:53
  75.1 15.7 %all_gather.30 = bf16[512,128]{1,0:T(8,128)(2,1)S(1)} all-gather(bf16[32,128]{1,0:T(8,128)(2,1)S(1)} %copy-done.5), channel_id=1, replica_groups=mesh['ctx'=16,'tp'=8] {'ctx'}, dimensions={0}, use_global_device_ids=true | all-gather | bytes 139264 | tf_op jit(solution)/shard_map/all_gather | solution.py:126
  90.9 16.9 %all_gather.31 = bf16[512,128]{1,0:T(8,128)(2,1)S(1)} all-gather(bf16[32,128]{1,0:T(8,128)(2,1)S(1)} %copy-done.6), channel_id=1, replica_groups=mesh['ctx'=16,'tp'=8] {'ctx'}, dimensions={0}, use_global_device_ids=true | all-gather | bytes 139264 | tf_op jit(solution)/shard_map/all_gather | solution.py:127
  107.7 10.9 %while.61 = (s32[]{:T(128)}, f32[8,32]{1,0:T(8,128)S(1)}, f32[8,32]{1,0:T(8,128)S(1)}, f32[8,32,128]{2,1,0:T(8,128)}, bf16[8,32,128]{2,1,0:T(8,128)(2,1)S(1)}, /...) while((s32[]{:T(128)}, f32[8,32]{1,0:T(8,128)S(1)}, ...), condition=%wide.region_14.15_spmd.clone, body=%wide.region_11.14_spmd.clone.sunk | while | flops 8683458 | bytes 487873 | solution.py:53
  118.6 41.2 %all-reduce.3.cloned.1.call-done = bf16[2,1024,128]{2,1,0:T(8,128)(2,1)} async-done(((bf16[2,1024,128]{2,1,0:T(8,128)(2,1)}), bf16[2,1024,128]{2,1,0:T(8,128)(2,1)}) %all-reduce.3.cloned.1.call-update) | async-done | bytes 524304 | tf_op jit(solution)/shard_map/psum | solution.py:14
  161.7 19.6 %all-gather = f32[8192,8]{0,1:T(8,128)S(1)} all-gather(f32[512,8]{0,1:T(8,128)S(1)} %bitcast.245), channel_id=2, replica_groups=mesh['ctx'=16,'tp'=8] {'ctx'}, dimensions={0}, use_global_device_ids=true | all-gather | bytes 278528 | tf_op jit(solution)/shard_map/all_gather | solution.py:18
  181.4 20.1 %all-gather.1 = f32[8192,8]{0,1:T(8,128)S(1)} all-gather(f32[512,8]{0,1:T(8,128)S(1)} %bitcast.246), channel_id=3, replica_groups=mesh['ctx'=16,'tp'=8] {'ctx'}, dimensions={0}, use_global_device_ids=true | all-gather | bytes 278528 | tf_op jit(solution)/shard_map/all_gather | solution.py:18
  201.5 139.5 %all-gather.7.cloned.1.call-done = f32[16,512,1024]{2,1,0:T(8,128)} async-done(((f32[1,512,1024]{2,1,0:T(8,128)}), f32[16,512,1024]{2,1,0:T(8,128)}) %all-gather.7.cloned.1.call-update) | async-done | bytes 33554448 | tf_op jit(solution)/shard_map/all_gather | solution.py:18
  341.0 22.4 %slice.43 = f32[15,512,1024]{2,1,0:T(8,128)} slice(f32[16,512,1024]{2,1,0:T(8,128)} %all-gather.7.cloned.1.call-done), slice={[1:16], [0:512], [0:1024]} | slice | bytes 62914560 | tf_op jit(solution)/shard_map/slice | solution.py:20
  366.6 134.1 %while.60 = (s32[]{:T(128)}, f32[512,8]{0,1:T(8,128)S(1)}, f32[512,8]{0,1:T(8,128)S(1)}, f32[512,1024]{1,0:T(8,128)}, f32[15,512,8]{1,2,0:T(8,128)S(1)}, /*index...) while((s32[]{:T(128)}, f32[512,8]{0,1:T(8,128)S(1)}, f32[512,8]{0,1:T(8,128)S(1)}, ...), condition=%wide.region_10.11_spmd, body=%wide.region_9.10_spmd.sunk | while | flops 1597442 | bytes 23298168 | solution.py:21
  370.5 5.1 fusion.106
  379.4 5.1 fusion.106
  388.3 5.1 fusion.106
  397.3 5.1 fusion.106
  406.2 5.1 fusion.106
  415.2 5.1 fusion.106
  450.9 5.1 fusion.106
  459.9 5.1 fusion.106
  468.8 5.1 fusion.106
  477.8 5.1 fusion.106
  486.7 5.1 fusion.106
  501.2 10.0 %fusion.61 = f32[32,8192]{1,0:T(8,128)} fusion(bf16[1024,8192]{1,0:T(8,128)(2,1)} %param.23, f32[4,8,8,128]{3,2,1,0:T(8,128)S(1)} %bitcast.233, f32[4,8,8,128]{3,2,1,0:T(8,128)S(1)} %bitcast.232, f32[512,1024]{1,0:T(8,128)} %get-tuple-element.223, s32[]{:T(128)S(6)} %select_n.53, f32[8,32,128]{2,1,0:T(8,128)} %get-tuple-element.226, ...), kind=kOutput, calls=%fused_computation.80 | convolution fusion | flops 537100288 | bytes 18353156 | tf_op jit(solution)/shard_map/dot_general | solution.py:138
  511.3 74.0 %while.58 = (s32[]{:T(128)}, f32[8,1024]{1,0:T(8,128)S(1)}, f32[8,1024,128]{2,1,0:T(8,128)}, bf16[8,1024,128]{1,2,0:T(8,128)(2,1)}, bf16[1,2048,128]{2,1,0:T(8,1...) while((s32[]{:T(128)}, f32[8,1024]{1,0:T(8,128)S(1)}, ...), condition=%wide.region_4.5_spmd, body=%wide.region_1.4_spmd.sunk | while | flops 1101002752 | bytes 33317984 | solution.py:53
  (276 shorter events, 205.9 us)
Async XLA Ops:
  7.2 37.2 %copy-start.1 = (bf16[1024,128]{1,0:T(8,128)(2,1)S(1)}, bf16[1024,128]{1,0:T(8,128)(2,1)}, u32[]{:S(2)}) copy-start(bf16[1024,128]{1,0:T(8,128)(2,1)} %param.17) | copy-start | bytes 786436
  7.2 37.2 %copy-start.2 = (bf16[1024,128]{1,0:T(8,128)(2,1)S(1)}, bf16[1024,128]{1,0:T(8,128)(2,1)}, u32[]{:S(2)}) copy-start(bf16[1024,128]{1,0:T(8,128)(2,1)} %param.18) | copy-start | bytes 786436
  7.2 35.6 %all-gather.5.cloned.1.call-start = ((), (), s32[]{:S(2)}) async-start(), calls=%async_computation.2 | async-start | bytes 1114112 | tf_op jit(solution)/shard_map/all_gather | solution.py:114
  7.9 151.9 %all-reduce.3.cloned.1.call-start = ((), (), s32[]{:S(2)}) async-start(), calls=%async_computation.1 | async-start | bytes 1048576 | tf_op jit(solution)/shard_map/psum | solution.py:14
  9.9 331.1 %all-gather.7.cloned.1.call-start = ((), (), s32[]{:S(2)}) async-start(), calls=%async_computation.3 | async-start | bytes 35651584 | tf_op jit(solution)/shard_map/all_gather | solution.py:18
  68.5 521.0 %reduce-scatter.2.cloned.1.call-start = ((), (), s32[]{:S(2)}) async-start(), calls=%async_computation.4 | async-start | bytes 1179648 | tf_op jit(solution)/shard_map/reduce_scatter | solution.py:139
  71.1 4.0 copy-start.5
  71.1 19.7 %copy-start.6 = (bf16[32,128]{1,0:T(8,128)(2,1)S(1)}, bf16[32,128]{1,0:T(8,128)(2,1)}, u32[]{:S(2)}) copy-start(bf16[32,128]{1,0:T(8,128)(2,1)} %param.21) | copy-start | bytes 24580
  368.9 1.6 copy-start
  377.8 1.6 copy-start
  386.7 1.6 copy-start
  395.7 1.6 copy-start
  404.6 1.6 copy-start
  413.6 1.6 copy-start
  422.5 1.6 copy-start
  431.5 1.6 copy-start
  440.4 1.6 copy-start
  449.3 1.6 copy-start
  458.3 1.6 copy-start
  467.2 1.6 copy-start
  476.2 1.6 copy-start
  485.1 1.6 copy-start
  494.1 1.6 copy-start
  501.2 10.1 %copy-start.3 = (bf16[1,2048,128]{2,1,0:T(8,128)(2,1)S(1)}, bf16[1,2048,128]{2,1,0:T(8,128)(2,1)}, u32[]{:S(2)}) copy-start(bf16[1,2048,128]{2,1,0:T(8,128)(2,1)} %get-tuple-element.716) | copy-start | bytes 1572868
  (1 other events, 0.8 us)
Sparse Core Ops, SparseCore 0:
  9.7 33.0 all-gather.4
  45.3 114.4 all-reduce.2
  161.5 179.4 all-gather.6
  511.4 72.9 reduce-scatter.1
where the time goes:
time: 600 us; the launch traced here: 596 us
  waiting for transfers between devices  214 us (36%)
  other arithmetic  114 us (19%)
  local copies, waits for them, and re-layouts  97.7 us (16%)
  matrix products  82.2 us (14%)
  blocking collectives  72.4 us (12%)
  between operations  14.7 us (2%)
    all_gather x1, waiting for transfers between devices, joined(): pieces = jax.tree.map(lambda part: lax.all_gather(part, axis), value)  139 us
    add x15, other arithmetic, combine(): earlier[2] * spread(first_factor, width)  76.5 us
    dot_general x24, matrix products, one_head(): jnp.dot(weights.astype(jnp.bfloat16), head_values, preferred_element_type...  42.8 us
    psum x1, waiting for transfers between devices, spread_2(): return lax.psum(block, axis)  41.2 us
    all_gather x2, blocking collectives, joined(): pieces = jax.tree.map(lambda part: lax.all_gather(part, axis), value)  39.7 us
    broadcast_in_dim x32, local copies, waits for them, and re-layouts, spread(): return jnp.repeat(factor, width // factor.shape[1], axis=1)  38.6 us
    all_gather x1, waiting for transfers between devices, on_device(): all_queries = lax.all_gather(resp_queries, 'ctx', axis=0, tiled=True)  32.9 us
    reduce_sum x24, other arithmetic, one_head(): row_sum = jnp.sum(weights, axis=1)  29.5 us
  transfers between devices with their start and end apart: 4, of which 3 were waited for; matrix products, arithmetic and copies ran while one was open for 21% of the time, Pallas kernels for 0%

commit v1 on v0

v1 whole, which is shorter than its diff:
```python
import functools

import jax
import jax.numpy as jnp
from jax import lax
from jax.experimental import pallas as pl
from jax.experimental.pallas import tpu as pltpu
from jax.sharding import PartitionSpec as P

HEAD_WIDTH = 128
NEGATIVE = -1e30
SCALE = HEAD_WIDTH ** (-0.5)
INTERPRET = False


def _dot_t(a, b):
    return lax.dot_general(a, b, (((1,), (1,)), ((), ())), preferred_element_type=jnp.float32)


def _ctx_kernel(flag_ref, q_ref, ka_ref, va_ref, ko_ref, vo_ref, o_ref):
    tq = q_ref.shape[0]
    block = ko_ref.shape[0]
    i = pl.program_id(1)
    q = q_ref[...]
    anchor_on = flag_ref[0] > 0
    s_a = _dot_t(q, ka_ref[...]) * SCALE
    s_o = _dot_t(q, ko_ref[...]) * SCALE
    rows = i * tq + lax.broadcasted_iota(jnp.int32, (tq, block), 0)
    cols = lax.broadcasted_iota(jnp.int32, (tq, block), 1)
    own_vis = cols <= rows
    s_a = jnp.where(anchor_on, s_a, NEGATIVE)
    s_o = jnp.where(own_vis, s_o, NEGATIVE)
    m = jnp.maximum(jnp.max(s_a, axis=1, keepdims=True), jnp.max(s_o, axis=1, keepdims=True))
    w_a = jnp.where(anchor_on, jnp.exp(s_a - m), 0.0)
    w_o = jnp.where(own_vis, jnp.exp(s_o - m), 0.0)
    total = jnp.sum(w_a, axis=1, keepdims=True) + jnp.sum(w_o, axis=1, keepdims=True)
    num = jnp.dot(w_a.astype(jnp.bfloat16), va_ref[...], preferred_element_type=jnp.float32)
    num = num + jnp.dot(w_o.astype(jnp.bfloat16), vo_ref[...], preferred_element_type=jnp.float32)
    o_ref[...] = num / total


def ctx_attention(flag, q, ka, va, ko, vo, tq=256):
    rows, width = q.shape
    heads = width // HEAD_WIDTH
    block = ko.shape[0]
    kv_spec = pl.BlockSpec((block, HEAD_WIDTH), lambda h, i, f: (0, 0))
    grid_spec = pltpu.PrefetchScalarGridSpec(
        num_scalar_prefetch=1,
        grid=(heads, rows // tq),
        in_specs=[
            pl.BlockSpec((tq, HEAD_WIDTH), lambda h, i, f: (i, h)),
            kv_spec, kv_spec, kv_spec, kv_spec,
        ],
        out_specs=pl.BlockSpec((tq, HEAD_WIDTH), lambda h, i, f: (i, h)),
    )
    return pl.pallas_call(
        _ctx_kernel,
        grid_spec=grid_spec,
        out_shape=jax.ShapeDtypeStruct((rows, width), jnp.float32),
        interpret=INTERPRET,
    )(flag, q, ka, va, ko, vo)


def _part_kernel(q_ref, k_ref, v_ref, num_ref, m_ref, l_ref):
    heads = q_ref.shape[1] // HEAD_WIDTH
    k = k_ref[...]
    v = v_ref[...]
    for j in range(heads):
        cols = slice(j * HEAD_WIDTH, (j + 1) * HEAD_WIDTH)
        s = _dot_t(q_ref[:, cols], k) * SCALE
        m = jnp.max(s, axis=1, keepdims=True)
        w = jnp.exp(s - m)
        m_ref[:, j:j + 1] = m
        l_ref[:, j:j + 1] = jnp.sum(w, axis=1, keepdims=True)
        num_ref[:, cols] = jnp.dot(w.astype(jnp.bfloat16), v, preferred_element_type=jnp.float32)


def part_attention(q, k, v, tq=128):
    rows = q.shape[0]
    width = q.shape[1]
    heads = width // HEAD_WIDTH
    block = k.shape[0]
    kv_spec = pl.BlockSpec((block, HEAD_WIDTH), lambda i: (0, 0))
    stat_spec = pl.BlockSpec((tq, heads), lambda i: (i, 0))
    return pl.pallas_call(
        _part_kernel,
        grid=(rows // tq,),
        in_specs=[pl.BlockSpec((tq, width), lambda i: (i, 0)), kv_spec, kv_spec],
        out_specs=[pl.BlockSpec((tq, width), lambda i: (i, 0)), stat_spec, stat_spec],
        out_shape=[
            jax.ShapeDtypeStruct((rows, width), jnp.float32),
            jax.ShapeDtypeStruct((rows, heads), jnp.float32),
            jax.ShapeDtypeStruct((rows, heads), jnp.float32),
        ],
        interpret=INTERPRET,
    )(q, k, v)


def on_device(
    ctx_queries,
    context_key_rows,
    context_value_rows,
    resp_queries,
    resp_keys,
    response_value_rows,
    split_index,
    out_weight,
):
    device = lax.axis_index("ctx")
    n_ctx = lax.axis_size("ctx")
    width = resp_queries.shape[1]
    heads = width // HEAD_WIDTH
    resp_dev = resp_queries.shape[0]

    packed = jnp.concatenate([resp_queries, resp_keys, response_value_rows], axis=1)
    gathered = lax.all_gather(packed, "ctx", axis=0, tiled=True)
    all_q = gathered[:, :width]
    all_k = gathered[:, width:width + HEAD_WIDTH]
    all_v = gathered[:, width + HEAD_WIDTH:]

    num, mx, tot = part_attention(all_q, context_key_rows, context_value_rows)
    state = jnp.concatenate([mx, tot, num], axis=1)
    state = lax.all_to_all(state, "ctx", 0, 0, tiled=True)
    state = state.reshape(n_ctx, resp_dev, -1)
    m_s = state[:, :, :heads]
    l_s = state[:, :, heads:2 * heads]
    num_s = state[:, :, 2 * heads:].reshape(n_ctx, resp_dev, heads, HEAD_WIDTH)

    own_rows = device * resp_dev + jnp.arange(resp_dev, dtype=jnp.int32)
    key_pos = jnp.arange(all_k.shape[0], dtype=jnp.int32)
    boundary = split_index[0]
    seen = (key_pos[None, :] <= own_rows[:, None]) & (
        (key_pos[None, :] < boundary) == (own_rows[:, None] < boundary)
    )
    q_own = resp_queries.reshape(resp_dev, heads, HEAD_WIDTH)
    s_r = jnp.einsum("rhd,kd->rhk", q_own, all_k, preferred_element_type=jnp.float32) * SCALE
    s_r = jnp.where(seen[:, None, :], s_r, NEGATIVE)
    m_r = jnp.max(s_r, axis=2)
    w_r = jnp.where(seen[:, None, :], jnp.exp(s_r - m_r[:, :, None]), 0.0)
    l_r = jnp.sum(w_r, axis=2)
    num_r = jnp.einsum(
        "rhk,kd->rhd", w_r.astype(jnp.bfloat16), all_v, preferred_element_type=jnp.float32
    )

    top = jnp.maximum(jnp.max(m_s, axis=0), m_r)
    f_s = jnp.exp(m_s - top[None])
    f_r = jnp.exp(m_r - top)
    total = jnp.sum(l_s * f_s, axis=0) + l_r * f_r
    numer = jnp.sum(num_s * f_s[..., None], axis=0) + num_r * f_r[..., None]
    attended = (numer / total[..., None]).reshape(resp_dev, width).astype(jnp.bfloat16)
    projected = jnp.dot(attended, out_weight, preferred_element_type=jnp.float32)
    resp_out = lax.psum_scatter(projected, "tp", scatter_dimension=1, tiled=True)

    anchor = jnp.stack([context_key_rows, context_value_rows])
    anchor = jnp.where(device == 0, anchor, jnp.zeros_like(anchor))
    anchor = lax.psum(anchor, "ctx")
    flag = (device > 0).astype(jnp.int32).reshape(1)
    ctx_out = ctx_attention(
        flag, ctx_queries, anchor[0], anchor[1], context_key_rows, context_value_rows
    )
    return (ctx_out, resp_out)


def solution(mesh):
    placed = (
        P("ctx", "tp"),
        P("ctx", "tp"),
        P("ctx", "tp"),
        P("ctx", "tp"),
        P("ctx", "tp"),
        P("ctx", "tp"),
        P(),
        P("tp", None),
    )
    return jax.shard_map(
        on_device,
        mesh=mesh,
        in_specs=placed,
        out_specs=(P("ctx", "tp"), P("ctx", "tp")),
        check_vma=False,
    )
```

time: 600 us -> 286 us (0.48)
  other arithmetic: 114 us -> 5.11 us
  local copies, waits for them, and re-layouts: 97.7 us -> 13.7 us
  blocking collectives: 72.4 us -> 0 us
  matrix products: 82.2 us -> 12.2 us
  Pallas kernels: 0 us -> 59.7 us
  waiting for transfers between devices: 214 us -> 174 us
    all_gather x2 -> x1, waiting for transfers between devices: 172 us -> 35 us  [on_device(): gathered = lax.all_gather(packed, 'ctx', axis=0, tiled=True)]
    add x31 -> x2, other arithmetic: 76.8 us -> 0.02 us  [the longest x1 0.01 us: on_device(): total = jnp.sum(l_s * f_s, axis=0) + l_r * f_r]
    all_gather x4 -> x0, blocking collectives: 72.4 us -> none  [the longest x2 39.7 us: joined(): pieces = jax.tree.map(lambda part: lax.all_gather(part, axis), value)]
    dot_general x48 -> x2, matrix products: 72.2 us -> 2.4 us  [the longest x1 1.21 us: on_device(): jnp.einsum('rhd,kd->rhk', q_own, all_k, preferred_element_type=jnp.float32)]
    pallas_call x0 -> x2, Pallas kernels: none -> 59.7 us  [the longest x1 45.8 us: ctx_attention(): pl.pallas_call(_ctx_kernel, grid_spec=grid_spec, out_shape=jax.ShapeDtype...]
    broadcast_in_dim x32 -> x0, local copies, waits for them, and re-layouts: 38.6 us -> none  [spread(): return jnp.repeat(factor, width // factor.shape[1], axis=1)]
    reduce_scatter x1, waiting for transfers between devices: 0.01 us -> 35.5 us  [on_device(): lax.psum_scatter(projected, 'tp', scatter_dimension=1, tiled=True)]
    psum x1, waiting for transfers between devices: 41.2 us -> 76.4 us  [on_device(): anchor = lax.psum(anchor, 'ctx')]
  transfers between devices with their start and end apart: 4 -> 4, of which waited for: 3 -> 4; matrix products, arithmetic and copies ran while one was open for 21% -> 8% of each run, Pallas kernels for 0% -> 16%
where the time goes in v1:
time: 286 us; the launch traced here: 284 us
  waiting for transfers between devices  174 us (61%)
  Pallas kernels  59.7 us (21%)
  between operations  14.5 us (5%)
  local copies, waits for them, and re-layouts  13.7 us (5%)
  matrix products  12.2 us (4%)
  starting transfers between devices  5.63 us (2%)
  other arithmetic  5.11 us (2%)
    psum x1, waiting for transfers between devices, on_device(): anchor = lax.psum(anchor, 'ctx')  76.4 us
    pallas_call x1, Pallas kernels, ctx_attention(): pl.pallas_call(_ctx_kernel, grid_spec=grid_spec, out_shape=jax.ShapeDtype...  45.8 us
    reduce_scatter x1, waiting for transfers between devices, on_device(): lax.psum_scatter(projected, 'tp', scatter_dimension=1, tiled=True)  35.5 us
    all_gather x1, waiting for transfers between devices, on_device(): gathered = lax.all_gather(packed, 'ctx', axis=0, tiled=True)  35 us
    all_to_all x1, waiting for transfers between devices, on_device(): state = lax.all_to_all(state, 'ctx', 0, 0, tiled=True)  26.7 us
    pallas_call x1, Pallas kernels, part_attention(): pl.pallas_call(_part_kernel, grid=(rows // tq,), in_specs=[pl.BlockSpec((...  13.9 us
    dot_general x1, matrix products, on_device(): jnp.dot(attended, out_weight, preferred_element_type=jnp.float32)  9.8 us
  transfers between devices with their start and end apart: 4, of which 4 were waited for; matrix products, arithmetic and copies ran while one was open for 8% of the time, Pallas kernels for 16%

profile of v1, /device:TPU:22, one launch (start us, length us, event | category | flops | bytes accessed | tf_op | source)
XLA Modules:
  0.0 284.4 jit_solution(9229167886156084075)
XLA Ops:
  7.2 1.5 pad_maximum_fusion
  8.8 35.0 %all-gather.2.cloned.1.call-done = bf16[512,1280]{1,0:T(8,128)(2,1)} async-done(((bf16[32,1280]{1,0:T(8,128)(2,1)}), bf16[512,1280]{1,0:T(8,128)(2,1)}) %all-gather.2.cloned.1.call-update) | async-done | bytes 1310736 | tf_op jit(solution)/shard_map/all_gather | solution.py:116
  43.7 2.3 slice.34.q_ref
  46.0 13.9 %shard_map.96 = (f32[512,1024]{1,0:T(8,128)}, f32[512,8]{1,0:T(8,128)}, f32[512,8]{1,0:T(8,128)}) custom-call(bf16[512,1024]{1,0:T(8,128)(2,1)} %slice.34.q_ref, bf16[1024,128]{1,0:T(8,128)(2,1)} %k_ref.1, bf16[1024,128]{1,0:T(8,128)(2,1)} %v_ref.1), custom_call_target="tpu_custom_call" | custom-call | tf_op jit(solution)/shard_map/pallas_call | solution.py:85
  59.9 4.4 %concatenate.7 = f32[512,1040]{1,0:T(8,128)} concatenate(f32[512,8]{1,0:T(8,128)} %get-tuple-element.5, f32[512,8]{1,0:T(8,128)} %get-tuple-element.6, f32[512,1024]{1,0:T(8,128)} %get-tuple-element.7), dimensions={1} | concatenate | bytes 4259840 | tf_op jit(solution)/shard_map/concatenate | solution.py:122
  64.3 5.5 %all-to-all-start = ((f32[16,32,1040]{2,1,0:T(8,128)}), f32[16,32,1040]{2,1,0:T(8,128)S(1)}, u32[]{:S(2)}, u32[]{:S(2)}) async-start(f32[16,32,1040]{2,1,0:T(8,128)} %bitcast.41), calls=%async_computation | async-start | bytes 4718592 | tf_op jit(solution)/shard_map/all_to_all | solution.py:123
  69.9 0.9 maximum_select_fusion
  71.5 0.1 fusion.15
  71.6 1.2 fusion.16
  72.8 0.2 fusion.6
  73.1 26.7 %all-to-all-done = f32[16,32,1040]{2,1,0:T(8,128)S(1)} async-done(((f32[16,32,1040]{2,1,0:T(8,128)}), f32[16,32,1040]{2,1,0:T(8,128)S(1)}, u32[]{:S(2)}, u32[]{:S(2)}) %all-to-all-start) | async-done | bytes 2129952 | tf_op jit(solution)/shard_map/all_to_all | solution.py:123
  99.9 0.1 copy.25
  100.0 0.1 fusion.8
  100.2 0.1 copy.27
  100.3 0.1 copy.29
  100.4 1.9 mul.45
  102.3 2.7 mul.46
  105.1 2.2 fusion
  107.3 1.2 fusion.5
  108.5 9.8 %fusion.10 = f32[32,8192]{1,0:T(8,128)} fusion(bf16[1024,8192]{1,0:T(8,128)(2,1)} %param.15, bf16[4,8,8,128]{3,2,1,0:T(8,128)(2,1)S(1)} %bitcast.46), kind=kOutput, calls=%fused_computation.23 | convolution fusion | flops 536870912 | bytes 17891328 | tf_op jit(solution)/shard_map/dot_general | solution.py:151
  118.4 76.4 %all-reduce.2.cloned.1.call-done = bf16[2,1024,128]{2,1,0:T(8,128)(2,1)} async-done(((bf16[2,1024,128]{2,1,0:T(8,128)(2,1)}), bf16[2,1024,128]{2,1,0:T(8,128)(2,1)}) %all-reduce.2.cloned.1.call-update) | async-done | bytes 524304 | tf_op jit(solution)/shard_map/psum | solution.py:156
  194.8 1.9 slice_bitcast_fusion
  196.6 45.8 %shard_map.95 = f32[1024,1024]{1,0:T(8,128)} custom-call(s32[1]{0:T(128)} %bitcast.flag_ref, bf16[1024,1024]{1,0:T(8,128)(2,1)} %q_ref.1, bf16[1024,128]{1,0:T(8,128)(2,1)} %get-tuple-element.15.ka_ref, bf16[1024,128]{1,0:T(8,128)(2,1)} %get-tuple-element.14.va_ref, bf16[1024,128]{1,0:T(8,128)(2,1)} %k_ref.1, bf16[1024,128]{1,0:T(8,128)(2,1)} %v_ref.1), custom_call_target="tpu_custom_call" | custom-call | tf_op jit(solution)/shard_map/pallas_call | solution.py:56
  242.4 35.5 %reduce-scatter.2.cloned.1.call-done = f32[32,1024]{1,0:T(8,128)} async-done(((f32[32,8192]{1,0:T(8,128)}), f32[32,1024]{1,0:T(8,128)}) %reduce-scatter.2.cloned.1.call-update) | async-done | bytes 131088 | tf_op jit(solution)/shard_map/reduce_scatter | solution.py:152
  (21 shorter events, 0.4 us)
Async XLA Ops:
  7.2 36.6 %all-gather.2.cloned.1.call-start = ((), (), s32[]{:S(2)}) async-start(), calls=%async_computation.3 | async-start | bytes 1392640 | tf_op jit(solution)/shard_map/all_gather | solution.py:116
  64.3 5.6 %copy-start = (bf16[1024,128]{1,0:T(8,128)(2,1)S(1)}, bf16[1024,128]{1,0:T(8,128)(2,1)}, u32[]{:S(2)}) copy-start(bf16[1024,128]{1,0:T(8,128)(2,1)} %v_ref.1) | copy-start | bytes 786436
  64.3 5.6 %copy-start.1 = (bf16[1024,128]{1,0:T(8,128)(2,1)S(1)}, bf16[1024,128]{1,0:T(8,128)(2,1)}, u32[]{:S(2)}) copy-start(bf16[1024,128]{1,0:T(8,128)(2,1)} %k_ref.1) | copy-start | bytes 786436
  64.3 7.3 %copy-start.2 = (bf16[32,1024]{1,0:T(8,128)(2,1)S(1)}, bf16[32,1024]{1,0:T(8,128)(2,1)}, u32[]{:S(2)}) copy-start(bf16[32,1024]{1,0:T(8,128)(2,1)} %param.11) | copy-start | bytes 196612
  64.3 35.5 %all-to-all-start = ((f32[16,32,1040]{2,1,0:T(8,128)}), f32[16,32,1040]{2,1,0:T(8,128)S(1)}, u32[]{:S(2)}, u32[]{:S(2)}) async-start(f32[16,32,1040]{2,1,0:T(8,128)} %bitcast.41), calls=%async_computation | async-start | bytes 4718592 | tf_op jit(solution)/shard_map/all_to_all | solution.py:123
  69.8 124.9 %all-reduce.2.cloned.1.call-start = ((), (), s32[]{:S(2)}) async-start(), calls=%async_computation.2 | async-start | bytes 1048576 | tf_op jit(solution)/shard_map/psum | solution.py:156
  70.8 207.1 %reduce-scatter.2.cloned.1.call-start = ((), (), s32[]{:S(2)}) async-start(), calls=%async_computation.4 | async-start | bytes 1179648 | tf_op jit(solution)/shard_map/reduce_scatter | solution.py:152
Sparse Core Ops, SparseCore 0:
  10.2 33.4 all-gather.1
  73.1 121.5 all-reduce.1
  198.9 78.9 reduce-scatter.1

commit v2 on v1

--- a/solution.py
+++ b/solution.py
@@ -96,6 +96,21 @@
     )(q, k, v)
 
 
+def gather_by_all_to_all(x, axis, n):
+    copies = jnp.broadcast_to(x[None], (n,) + x.shape)
+    return lax.all_to_all(copies, axis, 0, 0).reshape((n * x.shape[0],) + x.shape[1:])
+
+
+def broadcast_from_first(x, axis, device, n):
+    stride = n // 2
+    while stride >= 1:
+        pairs = [(s, s + stride) for s in range(0, n, 2 * stride)]
+        got = lax.ppermute(x, axis, pairs)
+        x = jnp.where(device % (2 * stride) == stride, got, x)
+        stride //= 2
+    return x
+
+
 def on_device(
     ctx_queries,
     context_key_rows,
@@ -113,7 +128,7 @@
     resp_dev = resp_queries.shape[0]
 
     packed = jnp.concatenate([resp_queries, resp_keys, response_value_rows], axis=1)
-    gathered = lax.all_gather(packed, "ctx", axis=0, tiled=True)
+    gathered = gather_by_all_to_all(packed, "ctx", n_ctx)
     all_q = gathered[:, :width]
     all_k = gathered[:, width:width + HEAD_WIDTH]
     all_v = gathered[:, width + HEAD_WIDTH:]
@@ -149,11 +164,13 @@
     numer = jnp.sum(num_s * f_s[..., None], axis=0) + num_r * f_r[..., None]
     attended = (numer / total[..., None]).reshape(resp_dev, width).astype(jnp.bfloat16)
     projected = jnp.dot(attended, out_weight, preferred_element_type=jnp.float32)
-    resp_out = lax.psum_scatter(projected, "tp", scatter_dimension=1, tiled=True)
+    n_tp = lax.axis_size("tp")
+    projected = projected.reshape(resp_dev, n_tp, -1).transpose(1, 0, 2)
+    resp_out = jnp.sum(lax.all_to_all(projected, "tp", 0, 0), axis=0)
 
-    anchor = jnp.stack([context_key_rows, context_value_rows])
-    anchor = jnp.where(device == 0, anchor, jnp.zeros_like(anchor))
-    anchor = lax.psum(anchor, "ctx")
+    anchor = broadcast_from_first(
+        jnp.stack([context_key_rows, context_value_rows]), "ctx", device, n_ctx
+    )
     flag = (device > 0).astype(jnp.int32).reshape(1)
     ctx_out = ctx_attention(
         flag, ctx_queries, anchor[0], anchor[1], context_key_rows, context_value_rows

time: 286 us -> 195 us (0.68)
  waiting for transfers between devices: 174 us -> 48.6 us
  local copies, waits for them, and re-layouts: 13.7 us -> 35.2 us
  starting transfers between devices: 5.63 us -> 25.2 us
  between operations: 14.5 us -> 1.5 us
  other arithmetic: 5.11 us -> 9.82 us
    psum x1 -> x0, waiting for transfers between devices: 76.4 us -> none  [on_device(): anchor = lax.psum(anchor, 'ctx')]
    reduce_scatter x1 -> x0, waiting for transfers between devices: 35.5 us -> none  [on_device(): lax.psum_scatter(projected, 'tp', scatter_dimension=1, tiled=True)]
    all_gather x1 -> x0, waiting for transfers between devices: 35 us -> none  [on_device(): gathered = lax.all_gather(packed, 'ctx', axis=0, tiled=True)]
    ppermute x0 -> x4, waiting for transfers between devices: none -> 33.1 us  [broadcast_from_first(): got = lax.ppermute(x, axis, pairs)]
    all_to_all x1, waiting for transfers between devices: 26.7 us -> 0.01 us  [on_device(): state = lax.all_to_all(state, 'ctx', 0, 0, tiled=True)]
    dot_general x0 -> x1, local copies, waits for them, and re-layouts: none -> 22.4 us  [on_device(): jnp.dot(attended, out_weight, preferred_element_type=jnp.float32)]
    all_to_all x0 -> x2, waiting for transfers between devices: none -> 15.5 us  [the longest x1 15.5 us: gather_by_all_to_all(): lax.all_to_all(copies, axis, 0, 0).reshape((n * x.shape[0],) + x.shape[1:])]
    all_to_all x0 -> x2, starting transfers between devices: none -> 13.8 us  [the longest x1 8.26 us: on_device(): resp_out = jnp.sum(lax.all_to_all(projected, 'tp', 0, 0), axis=0)]
  transfers between devices with their start and end apart: 4 -> 7, of which waited for: 4 -> 2; matrix products, arithmetic and copies ran while one was open for 8% -> 29% of each run, Pallas kernels for 16% -> 31%
where the time goes in v2:
time: 195 us; the launch traced here: 194 us
  Pallas kernels  59.7 us (31%)
  waiting for transfers between devices  48.6 us (25%)
  local copies, waits for them, and re-layouts  35.2 us (18%)
  starting transfers between devices  25.2 us (13%)
  matrix products  14.1 us (7%)
  other arithmetic  9.82 us (5%)
    pallas_call x1, Pallas kernels, ctx_attention(): pl.pallas_call(_ctx_kernel, grid_spec=grid_spec, out_shape=jax.ShapeDtype...  45.8 us
    ppermute x4, waiting for transfers between devices, broadcast_from_first(): got = lax.ppermute(x, axis, pairs)  33.1 us
    dot_general x1, local copies, waits for them, and re-layouts, on_device(): jnp.dot(attended, out_weight, preferred_element_type=jnp.float32)  22.4 us
    all_to_all x1, waiting for transfers between devices, gather_by_all_to_all(): lax.all_to_all(copies, axis, 0, 0).reshape((n * x.shape[0],) + x.shape[1:])  15.5 us
    pallas_call x1, Pallas kernels, part_attention(): pl.pallas_call(_part_kernel, grid=(rows // tq,), in_specs=[pl.BlockSpec((...  13.9 us
    dot_general x1, matrix products, on_device(): jnp.dot(attended, out_weight, preferred_element_type=jnp.float32)  11.8 us
    all_to_all x1, starting transfers between devices, on_device(): resp_out = jnp.sum(lax.all_to_all(projected, 'tp', 0, 0), axis=0)  8.26 us
    all_to_all x1, starting transfers between devices, on_device(): state = lax.all_to_all(state, 'ctx', 0, 0, tiled=True)  6.02 us
  transfers between devices with their start and end apart: 7, of which 2 were waited for; matrix products, arithmetic and copies ran while one was open for 29% of the time, Pallas kernels for 31%

profile of v2, /device:TPU:22, one launch (start us, length us, event | category | flops | bytes accessed | tf_op | source)
XLA Modules:
  0.0 194.1 jit_solution(17822800123159305319)
XLA Ops:
  0.7 0.9 pad_maximum_fusion.1
  1.6 1.2 broadcast_in_dim.20
  2.8 5.5 %all-to-all-start = ((bf16[16,32,1280]{2,1,0:T(8,128)(2,1)}), bf16[16,32,1280]{2,1,0:T(8,128)(2,1)S(1)}, u32[]{:S(2)}, u32[]{:S(2)}) async-start(bf16[16,32,1280]{2,1,0:T(8,128)(2,1)} %broadcast_in_dim.20), calls=%async_computation | async-start | bytes 2621440 | tf_op jit(solution)/shard_map/all_to_all | solution.py:101
  9.8 15.5 %all-to-all-done = bf16[16,32,1280]{2,1,0:T(8,128)(2,1)S(1)} async-done(((bf16[16,32,1280]{2,1,0:T(8,128)(2,1)}), bf16[16,32,1280]{2,1,0:T(8,128)(2,1)S(1)}, u32[]{:S(2)}, u32[]{:S(2)}) %all-to-all-start) | async-done | bytes 1310752 | tf_op jit(solution)/shard_map/all_to_all | solution.py:101
  25.3 1.2 slice.34.q_ref
  26.6 13.9 %shard_map.96 = (f32[512,1024]{1,0:T(8,128)}, f32[512,8]{1,0:T(8,128)}, f32[512,8]{1,0:T(8,128)}) custom-call(bf16[512,1024]{1,0:T(8,128)(2,1)} %slice.34.q_ref, bf16[1024,128]{1,0:T(8,128)(2,1)} %k_ref.1, bf16[1024,128]{1,0:T(8,128)(2,1)} %v_ref.1), custom_call_target="tpu_custom_call" | custom-call | tf_op jit(solution)/shard_map/pallas_call | solution.py:85
  40.4 4.4 %concatenate.7 = f32[512,1040]{1,0:T(8,128)} concatenate(f32[512,8]{1,0:T(8,128)} %get-tuple-element.5, f32[512,8]{1,0:T(8,128)} %get-tuple-element.6, f32[512,1024]{1,0:T(8,128)} %get-tuple-element.7), dimensions={1} | concatenate | bytes 4259840 | tf_op jit(solution)/shard_map/concatenate | solution.py:137
  44.9 6.0 %all-to-all-start.1 = ((f32[16,32,1040]{2,1,0:T(8,128)}), f32[16,32,1040]{2,1,0:T(8,128)S(1)}, u32[]{:S(2)}, u32[]{:S(2)}) async-start(f32[16,32,1040]{2,1,0:T(8,128)} %bitcast.45), calls=%async_computation.1 | async-start | bytes 4718592 | tf_op jit(solution)/shard_map/all_to_all | solution.py:138
  50.9 0.9 broadcast_select_fusion
  51.8 1.3 collective-permute-start.1
  53.8 33.1 %collective-permute-done.1 = bf16[2,1024,128]{2,1,0:T(8,128)(2,1)} collective-permute-done((bf16[2,1024,128]{2,1,0:T(8,128)(2,1)}, bf16[2,1024,128]{2,1,0:T(8,128)(2,1)}, u32[]{:S(2)}, u32[]{:S(2)}) %collective-permute-start.1) | collective-permute-done | bytes 524320 | tf_op jit(solution)/shard_map/ppermute | solution.py:108
  86.9 1.9 broadcast_select_fusion.1
  88.8 1.3 collective-permute-start.2
  90.2 22.4 %copy.34 = bf16[8192,1024]{1,0:T(8,128)(2,1)} copy(bf16[8192,1024]{0,1:T(8,128)(2,1)} %bitcast.44) | data formatting | bytes 33554432 | tf_op jit(solution)/shard_map/dot_general | solution.py:166
  112.6 1.2 fusion.13
  114.7 1.1 broadcast_select_fusion.2
  115.8 2.1 %collective-permute-start.3 = (bf16[2,1024,128]{2,1,0:T(8,128)(2,1)S(1)}, bf16[2,1024,128]{2,1,0:T(8,128)(2,1)}, u32[]{:S(2)}, u32[]{:S(2)}) collective-permute-start(bf16[2,1024,128]{2,1,0:T(8,128)(2,1)S(1)} %broadcast_select_fusion.2), channel_id=1, source_target_pairs={{0,8},{16,24},{32,40},{48,56},{64,72},{80,88},{96,104},{112,120},{... | collective-permute-start | bytes 1572872 | tf_op jit(solution)/shard_map/ppermute | solution.py:108
  118.5 1.9 mul.45
  120.4 2.7 %mul.46 = f32[16,32,1024]{2,1,0:T(8,128)} reshape(f32[16,32,8,128]{3,2,1,0:T(8,128)} %mul.45) | data formatting | bytes 4194304 | tf_op jit(solution)/shard_map/mul | solution.py:164
  123.1 2.2 %fusion = f32[32,1024]{1,0:T(8,128)S(1)} fusion(f32[16,32,1024]{2,1,0:T(8,128)} %mul.46, f32[16,32,1040]{2,1,0:T(8,128)S(1)} %all-to-all-done.1), kind=kLoop, calls=%fused_computation.1 | loop fusion | flops 1015808 | bytes 4325376 | tf_op jit(solution)/shard_map/reduce_sum | solution.py:164
  125.4 1.2 fusion.5
  126.7 11.8 %convolution_bitcast_fusion = f32[8,32,1024]{2,1,0:T(8,128)} fusion(bf16[32,1024,1]{1,0,2:T(8,128)(2,1)S(1)} %reshape.113, bf16[8,1024,1024]{2,1,0:T(8,128)(2,1)} %bitcast.43), kind=kOutput, calls=%fused_computation.2 | convolution fusion | flops 536870912 | bytes 17891328 | tf_op jit(solution)/shard_map/dot_general | solution.py:166
  138.4 8.3 %all-to-all-start.2 = ((f32[8,32,1024]{2,1,0:T(8,128)}), f32[8,32,1024]{2,1,0:T(8,128)S(1)}, u32[]{:S(2)}, u32[]{:S(2)}) async-start(f32[8,32,1024]{2,1,0:T(8,128)} %convolution_bitcast_fusion), calls=%async_computation.2 | async-start | bytes 2097152 | tf_op jit(solution)/shard_map/all_to_all | solution.py:169
  147.6 45.8 %shard_map.95 = f32[1024,1024]{1,0:T(8,128)} custom-call(s32[1]{0:T(128)} %bitcast.flag_ref, bf16[1024,1024]{1,0:T(8,128)(2,1)} %q_ref.1, bf16[1024,128]{1,0:T(8,128)(2,1)} %get-tuple-element.15.ka_ref, bf16[1024,128]{1,0:T(8,128)(2,1)} %get-tuple-element.14.va_ref, bf16[1024,128]{1,0:T(8,128)(2,1)} %k_ref.1, bf16[1024,128]{1,0:T(8,128)(2,1)} %v_ref.1), custom_call_target="tpu_custom_call" | custom-call | tf_op jit(solution)/shard_map/pallas_call | solution.py:56
  (40 shorter events, 4.7 us)
Async XLA Ops:
  0.6 7.7 %copy-start.2 = (bf16[1024,128]{1,0:T(8,128)(2,1)S(1)}, bf16[1024,128]{1,0:T(8,128)(2,1)}, u32[]{:S(2)}) copy-start(bf16[1024,128]{1,0:T(8,128)(2,1)} %k_ref.1) | copy-start | bytes 786436
  0.6 7.7 %copy-start = (bf16[1024,128]{1,0:T(8,128)(2,1)S(1)}, bf16[1024,128]{1,0:T(8,128)(2,1)}, u32[]{:S(2)}) copy-start(bf16[1024,128]{1,0:T(8,128)(2,1)} %v_ref.1) | copy-start | bytes 786436
  2.8 22.6 %all-to-all-start = ((bf16[16,32,1280]{2,1,0:T(8,128)(2,1)}), bf16[16,32,1280]{2,1,0:T(8,128)(2,1)S(1)}, u32[]{:S(2)}, u32[]{:S(2)}) async-start(bf16[16,32,1280]{2,1,0:T(8,128)(2,1)} %broadcast_in_dim.20), calls=%async_computation | async-start | bytes 2621440 | tf_op jit(solution)/shard_map/all_to_all | solution.py:101
  9.1 41.8 %collective-permute-start = (bf16[2,1024,128]{2,1,0:T(8,128)(2,1)}, bf16[2,1024,128]{2,1,0:T(8,128)(2,1)S(1)}, u32[]{:S(2)}, u32[]{:S(2)}) collective-permute-start(bf16[2,1024,128]{2,1,0:T(8,128)(2,1)} %pad_maximum_fusion), channel_id=1, source_target_pairs={{0,64},{1,65},{2,66},{3,67},{4,68},{5,69},{6,70},{7,71}} | collective-permute-start | bytes 1572872 | tf_op jit(solution)/shard_map/ppermute | solution.py:108
  25.3 19.5 %copy-start.4 = (bf16[16,32,1280]{2,1,0:T(8,128)(2,1)}, bf16[16,32,1280]{2,1,0:T(8,128)(2,1)S(1)}, u32[]{:S(2)}) copy-start(bf16[16,32,1280]{2,1,0:T(8,128)(2,1)S(1)} %all-to-all-done) | copy-start | bytes 3932164
  44.9 6.0 %copy-start.1 = (bf16[1024,128]{1,0:T(8,128)(2,1)S(1)}, bf16[1024,128]{1,0:T(8,128)(2,1)}, u32[]{:S(2)}) copy-start(bf16[1024,128]{1,0:T(8,128)(2,1)} %v_ref.1) | copy-start | bytes 786436
  44.9 6.0 %copy-start.3 = (bf16[1024,128]{1,0:T(8,128)(2,1)S(1)}, bf16[1024,128]{1,0:T(8,128)(2,1)}, u32[]{:S(2)}) copy-start(bf16[1024,128]{1,0:T(8,128)(2,1)} %k_ref.1) | copy-start | bytes 786436
  44.9 73.0 %all-to-all-start.1 = ((f32[16,32,1040]{2,1,0:T(8,128)}), f32[16,32,1040]{2,1,0:T(8,128)S(1)}, u32[]{:S(2)}, u32[]{:S(2)}) async-start(f32[16,32,1040]{2,1,0:T(8,128)} %bitcast.45), calls=%async_computation.1 | async-start | bytes 4718592 | tf_op jit(solution)/shard_map/all_to_all | solution.py:138
  51.8 35.1 %collective-permute-start.1 = (bf16[2,1024,128]{2,1,0:T(8,128)(2,1)}, bf16[2,1024,128]{2,1,0:T(8,128)(2,1)}, u32[]{:S(2)}, u32[]{:S(2)}) collective-permute-start(bf16[2,1024,128]{2,1,0:T(8,128)(2,1)} %broadcast_select_fusion), channel_id=1, source_target_pairs={{0,32},{64,96},{1,33},{65,97},{2,34},{66,98},{3,35},{67,99},{4,36}... | collective-permute-start | bytes 1572872 | tf_op jit(solution)/shard_map/ppermute | solution.py:108
  88.8 25.9 %collective-permute-start.2 = (bf16[2,1024,128]{2,1,0:T(8,128)(2,1)}, bf16[2,1024,128]{2,1,0:T(8,128)(2,1)S(1)}, u32[]{:S(2)}, u32[]{:S(2)}) collective-permute-start(bf16[2,1024,128]{2,1,0:T(8,128)(2,1)} %broadcast_select_fusion.1), channel_id=1, source_target_pairs={{0,16},{32,48},{64,80},{96,112},{1,17},{33,49},{65,81},{97,113},{2... | collective-permute-start | bytes 1572872 | tf_op jit(solution)/shard_map/ppermute | solution.py:108
  90.2 22.4 %copy-start.6 = (bf16[32,1024]{1,0:T(8,128)(2,1)S(1)}, bf16[32,1024]{1,0:T(8,128)(2,1)}, u32[]{:S(2)}) copy-start(bf16[32,1024]{1,0:T(8,128)(2,1)} %param.11) | copy-start | bytes 196612
  115.8 30.9 %collective-permute-start.3 = (bf16[2,1024,128]{2,1,0:T(8,128)(2,1)S(1)}, bf16[2,1024,128]{2,1,0:T(8,128)(2,1)}, u32[]{:S(2)}, u32[]{:S(2)}) collective-permute-start(bf16[2,1024,128]{2,1,0:T(8,128)(2,1)S(1)} %broadcast_select_fusion.2), channel_id=1, source_target_pairs={{0,8},{16,24},{32,40},{48,56},{64,72},{80,88},{96,104},{112,120},{... | collective-permute-start | bytes 1572872 | tf_op jit(solution)/shard_map/ppermute | solution.py:108
  123.1 2.3 %copy-start.5 = (bf16[32,8,512]{2,0,1:T(8,128)(2,1)S(1)}, bf16[32,8,512]{2,0,1:T(8,128)(2,1)}, u32[]{:S(2)}) copy-start(bf16[32,8,512]{2,0,1:T(8,128)(2,1)} %get-tuple-element.13) | copy-start | bytes 786436
  138.4 54.9 %all-to-all-start.2 = ((f32[8,32,1024]{2,1,0:T(8,128)}), f32[8,32,1024]{2,1,0:T(8,128)S(1)}, u32[]{:S(2)}, u32[]{:S(2)}) async-start(f32[8,32,1024]{2,1,0:T(8,128)} %convolution_bitcast_fusion), calls=%async_computation.2 | async-start | bytes 2097152 | tf_op jit(solution)/shard_map/all_to_all | solution.py:169

commit v3 on v2

v3 whole, which is shorter than its diff:
```python
import functools

import jax
import jax.numpy as jnp
from jax import lax
from jax.experimental import pallas as pl
from jax.experimental.pallas import tpu as pltpu
from jax.sharding import PartitionSpec as P

HEAD_WIDTH = 128
NEGATIVE = -1e30
SCALE = HEAD_WIDTH ** (-0.5)
INTERPRET = False


def _dot_t(a, b):
    return lax.dot_general(a, b, (((1,), (1,)), ((), ())), preferred_element_type=jnp.float32)


def _own_kernel(q_ref, k_ref, v_ref, st_ref):
    tq = q_ref.shape[0]
    width = q_ref.shape[1]
    heads = width // HEAD_WIDTH
    i = pl.program_id(0)
    rows = lax.broadcasted_iota(jnp.int32, (tq, tq), 0)
    cols = lax.broadcasted_iota(jnp.int32, (tq, tq), 1)
    diag_vis = cols <= rows
    start = pl.multiple_of(i * tq, tq)
    kd = k_ref[pl.ds(start, tq), :]
    vd = v_ref[pl.ds(start, tq), :]
    for j in range(heads):
        hc = slice(j * HEAD_WIDTH, (j + 1) * HEAD_WIDTH)
        q = q_ref[:, hc]
        s = jnp.where(diag_vis, _dot_t(q, kd) * SCALE, NEGATIVE)
        m = jnp.max(s, axis=1, keepdims=True)
        p = jnp.where(diag_vis, jnp.exp(s - m), 0.0)
        l = jnp.sum(p, axis=1, keepdims=True)
        acc = jnp.dot(p.astype(jnp.bfloat16), vd, preferred_element_type=jnp.float32)

        def body(t, carry, q=q):
            m, l, acc = carry
            at = pl.multiple_of(t * tq, tq)
            s = _dot_t(q, k_ref[pl.ds(at, tq), :]) * SCALE
            m_new = jnp.maximum(m, jnp.max(s, axis=1, keepdims=True))
            a = jnp.exp(m - m_new)
            p = jnp.exp(s - m_new)
            l = a * l + jnp.sum(p, axis=1, keepdims=True)
            acc = a * acc + jnp.dot(
                p.astype(jnp.bfloat16), v_ref[pl.ds(at, tq), :], preferred_element_type=jnp.float32
            )
            return m_new, l, acc

        m, l, acc = lax.fori_loop(0, i, body, (m, l, acc))
        st_ref[:, hc] = acc
        st_ref[:, width + j:width + j + 1] = m
        st_ref[:, width + heads + j:width + heads + j + 1] = l


def own_attention(q, k, v, tq=256):
    rows, width = q.shape
    heads = width // HEAD_WIDTH
    block = k.shape[0]
    kv_spec = pl.BlockSpec((block, HEAD_WIDTH), lambda i: (0, 0))
    return pl.pallas_call(
        _own_kernel,
        grid=(rows // tq,),
        in_specs=[pl.BlockSpec((tq, width), lambda i: (i, 0)), kv_spec, kv_spec],
        out_specs=pl.BlockSpec((tq, width + 2 * heads), lambda i: (i, 0)),
        out_shape=jax.ShapeDtypeStruct((rows, width + 2 * heads), jnp.float32),
        interpret=INTERPRET,
    )(q, k, v)


def _anchor_kernel(flag_ref, q_ref, ka_ref, va_ref, st_ref, o_ref):
    width = q_ref.shape[1]
    heads = width // HEAD_WIDTH
    on = flag_ref[0] > 0

    @pl.when(on)
    def _():
        ka = ka_ref[...]
        va = va_ref[...]
        for j in range(heads):
            hc = slice(j * HEAD_WIDTH, (j + 1) * HEAD_WIDTH)
            m_o = st_ref[:, width + j:width + j + 1]
            l_o = st_ref[:, width + heads + j:width + heads + j + 1]
            s = _dot_t(q_ref[:, hc], ka) * SCALE
            m = jnp.maximum(m_o, jnp.max(s, axis=1, keepdims=True))
            p = jnp.exp(s - m)
            a = jnp.exp(m_o - m)
            l = a * l_o + jnp.sum(p, axis=1, keepdims=True)
            num = a * st_ref[:, hc] + jnp.dot(
                p.astype(jnp.bfloat16), va, preferred_element_type=jnp.float32
            )
            o_ref[:, hc] = num / l

    @pl.when(jnp.logical_not(on))
    def _():
        for j in range(heads):
            hc = slice(j * HEAD_WIDTH, (j + 1) * HEAD_WIDTH)
            o_ref[:, hc] = st_ref[:, hc] / st_ref[:, width + heads + j:width + heads + j + 1]


def anchor_attention(flag, q, ka, va, st, tq=256):
    rows, width = q.shape
    block = ka.shape[0]
    kv_spec = pl.BlockSpec((block, HEAD_WIDTH), lambda i, f: (0, 0))
    grid_spec = pltpu.PrefetchScalarGridSpec(
        num_scalar_prefetch=1,
        grid=(rows // tq,),
        in_specs=[
            pl.BlockSpec((tq, width), lambda i, f: (i, 0)),
            kv_spec,
            kv_spec,
            pl.BlockSpec((tq, st.shape[1]), lambda i, f: (i, 0)),
        ],
        out_specs=pl.BlockSpec((tq, width), lambda i, f: (i, 0)),
    )
    return pl.pallas_call(
        _anchor_kernel,
        grid_spec=grid_spec,
        out_shape=jax.ShapeDtypeStruct((rows, width), jnp.float32),
        interpret=INTERPRET,
    )(flag, q, ka, va, st)


def _part_kernel(q_ref, k_ref, v_ref, st_ref):
    width = q_ref.shape[1]
    heads = width // HEAD_WIDTH
    k = k_ref[...]
    v = v_ref[...]
    for j in range(heads):
        hc = slice(j * HEAD_WIDTH, (j + 1) * HEAD_WIDTH)
        s = _dot_t(q_ref[:, hc], k) * SCALE
        m = jnp.max(s, axis=1, keepdims=True)
        w = jnp.exp(s - m)
        st_ref[:, width + j:width + j + 1] = m
        st_ref[:, width + heads + j:width + heads + j + 1] = jnp.sum(w, axis=1, keepdims=True)
        st_ref[:, hc] = jnp.dot(w.astype(jnp.bfloat16), v, preferred_element_type=jnp.float32)


def part_attention(q, k, v, tq=128):
    rows = q.shape[0]
    width = q.shape[1]
    heads = width // HEAD_WIDTH
    block = k.shape[0]
    kv_spec = pl.BlockSpec((block, HEAD_WIDTH), lambda i: (0, 0))
    return pl.pallas_call(
        _part_kernel,
        grid=(rows // tq,),
        in_specs=[pl.BlockSpec((tq, width), lambda i: (i, 0)), kv_spec, kv_spec],
        out_specs=pl.BlockSpec((tq, width + 2 * heads), lambda i: (i, 0)),
        out_shape=jax.ShapeDtypeStruct((rows, width + 2 * heads), jnp.float32),
        interpret=INTERPRET,
    )(q, k, v)


def gather_by_all_to_all(x, axis, n):
    copies = jnp.broadcast_to(x[None], (n,) + x.shape)
    return lax.all_to_all(copies, axis, 0, 0).reshape((n * x.shape[0],) + x.shape[1:])


def broadcast_from_first(x, axis, device, n):
    stride = n // 2
    while stride >= 1:
        pairs = [(s, s + stride) for s in range(0, n, 2 * stride)]
        got = lax.ppermute(x, axis, pairs)
        x = jnp.where(device % (2 * stride) == stride, got, x)
        stride //= 2
    return x


def on_device(
    ctx_queries,
    context_key_rows,
    context_value_rows,
    resp_queries,
    resp_keys,
    response_value_rows,
    split_index,
    out_weight,
):
    device = lax.axis_index("ctx")
    n_ctx = lax.axis_size("ctx")
    width = resp_queries.shape[1]
    heads = width // HEAD_WIDTH
    resp_dev = resp_queries.shape[0]

    packed = jnp.concatenate([resp_queries, resp_keys, response_value_rows], axis=1)
    gathered = gather_by_all_to_all(packed, "ctx", n_ctx)
    all_q = gathered[:, :width]
    all_k = gathered[:, width:width + HEAD_WIDTH]
    all_v = gathered[:, width + HEAD_WIDTH:]

    state = part_attention(all_q, context_key_rows, context_value_rows)
    state = lax.all_to_all(state, "ctx", 0, 0, tiled=True)
    state = state.reshape(n_ctx, resp_dev, -1)
    num_s = state[:, :, :width].reshape(n_ctx, resp_dev, heads, HEAD_WIDTH)
    m_s = state[:, :, width:width + heads]
    l_s = state[:, :, width + heads:]

    own_rows = device * resp_dev + jnp.arange(resp_dev, dtype=jnp.int32)
    key_pos = jnp.arange(all_k.shape[0], dtype=jnp.int32)
    boundary = split_index[0]
    seen = (key_pos[None, :] <= own_rows[:, None]) & (
        (key_pos[None, :] < boundary) == (own_rows[:, None] < boundary)
    )
    q_own = resp_queries.reshape(resp_dev, heads, HEAD_WIDTH)
    s_r = jnp.einsum("rhd,kd->rhk", q_own, all_k, preferred_element_type=jnp.float32) * SCALE
    s_r = jnp.where(seen[:, None, :], s_r, NEGATIVE)
    m_r = jnp.max(s_r, axis=2)
    w_r = jnp.where(seen[:, None, :], jnp.exp(s_r - m_r[:, :, None]), 0.0)
    l_r = jnp.sum(w_r, axis=2)
    num_r = jnp.einsum(
        "rhk,kd->rhd", w_r.astype(jnp.bfloat16), all_v, preferred_element_type=jnp.float32
    )

    top = jnp.maximum(jnp.max(m_s, axis=0), m_r)
    f_s = jnp.exp(m_s - top[None])
    f_r = jnp.exp(m_r - top)
    total = jnp.sum(l_s * f_s, axis=0) + l_r * f_r
    numer = jnp.sum(num_s * f_s[..., None], axis=0) + num_r * f_r[..., None]
    attended = (numer / total[..., None]).reshape(resp_dev, width).astype(jnp.bfloat16)
    projected = jnp.dot(attended, out_weight, preferred_element_type=jnp.float32)
    n_tp = lax.axis_size("tp")
    shares = lax.all_to_all(projected, "tp", 1, 0, tiled=True)
    resp_out = jnp.sum(shares.reshape(n_tp, resp_dev, -1), axis=0)

    own_state = own_attention(ctx_queries, context_key_rows, context_value_rows)
    anchor = broadcast_from_first(
        jnp.stack([context_key_rows, context_value_rows]), "ctx", device, n_ctx
    )
    flag = (device > 0).astype(jnp.int32).reshape(1)
    ctx_out = anchor_attention(flag, ctx_queries, anchor[0], anchor[1], own_state)
    return (ctx_out, resp_out)


def solution(mesh):
    placed = (
        P("ctx", "tp"),
        P("ctx", "tp"),
        P("ctx", "tp"),
        P("ctx", "tp"),
        P("ctx", "tp"),
        P("ctx", "tp"),
        P(),
        P("tp", None),
    )
    return jax.shard_map(
        on_device,
        mesh=mesh,
        in_specs=placed,
        out_specs=(P("ctx", "tp"), P("ctx", "tp")),
        check_vma=False,
    )
```

time: 195 us -> 207 us (1.062)
  Pallas kernels: 59.7 us -> 76.6 us
  local copies, waits for them, and re-layouts: 35.2 us -> 30.8 us
    pallas_call x1 -> x2, Pallas kernels: 45.8 us -> 62.7 us  [the longest x1 38.8 us: own_attention(): pl.pallas_call(_own_kernel, grid=(rows // tq,), in_specs=[pl.BlockSpec((t...]
    concatenate x1 -> x0, local copies, waits for them, and re-layouts: 4.44 us -> none  [on_device(): state = jnp.concatenate([mx, tot, num], axis=1)]
  transfers between devices with their start and end apart: 7 -> 7, of which waited for: 2 -> 2; matrix products, arithmetic and copies ran while one was open for 29% -> 25% of each run, Pallas kernels for 31% -> 37%
where the time goes in v3:
time: 207 us; the launch traced here: 206 us
  Pallas kernels  76.6 us (37%)
  waiting for transfers between devices  48.5 us (23%)
  local copies, waits for them, and re-layouts  30.8 us (15%)
  starting transfers between devices  25.2 us (12%)
  matrix products  14.1 us (7%)
  other arithmetic  9.46 us (5%)
    pallas_call x1, Pallas kernels, own_attention(): pl.pallas_call(_own_kernel, grid=(rows // tq,), in_specs=[pl.BlockSpec((t...  38.8 us
    ppermute x4, waiting for transfers between devices, broadcast_from_first(): got = lax.ppermute(x, axis, pairs)  33.1 us
    pallas_call x1, Pallas kernels, anchor_attention(): pl.pallas_call(_anchor_kernel, grid_spec=grid_spec, out_shape=jax.ShapeDt...  23.9 us
    dot_general x1, local copies, waits for them, and re-layouts, on_device(): jnp.dot(attended, out_weight, preferred_element_type=jnp.float32)  22.4 us
    all_to_all x1, waiting for transfers between devices, gather_by_all_to_all(): lax.all_to_all(copies, axis, 0, 0).reshape((n * x.shape[0],) + x.shape[1:])  15.5 us
    pallas_call x1, Pallas kernels, part_attention(): pl.pallas_call(_part_kernel, grid=(rows // tq,), in_specs=[pl.BlockSpec((...  13.9 us
    dot_general x1, matrix products, on_device(): jnp.dot(attended, out_weight, preferred_element_type=jnp.float32)  11.7 us
    all_to_all x1, starting transfers between devices, on_device(): shares = lax.all_to_all(projected, 'tp', 1, 0, tiled=True)  8.28 us
  transfers between devices with their start and end apart: 7, of which 2 were waited for; matrix products, arithmetic and copies ran while one was open for 25% of the time, Pallas kernels for 37%

profile of v3, /device:TPU:22, one launch (start us, length us, event | category | flops | bytes accessed | tf_op | source)
XLA Modules:
  0.0 206.2 jit_solution(864347608501193252)
XLA Ops:
  0.7 0.9 pad_maximum_fusion.1
  1.6 1.2 broadcast_in_dim.20
  2.8 5.5 %all-to-all-start = ((bf16[16,32,1280]{2,1,0:T(8,128)(2,1)}), bf16[16,32,1280]{2,1,0:T(8,128)(2,1)S(1)}, u32[]{:S(2)}, u32[]{:S(2)}) async-start(bf16[16,32,1280]{2,1,0:T(8,128)(2,1)} %broadcast_in_dim.20), calls=%async_computation | async-start | bytes 2621440 | tf_op jit(solution)/shard_map/all_to_all | solution.py:160
  9.9 15.5 %all-to-all-done = bf16[16,32,1280]{2,1,0:T(8,128)(2,1)S(1)} async-done(((bf16[16,32,1280]{2,1,0:T(8,128)(2,1)}), bf16[16,32,1280]{2,1,0:T(8,128)(2,1)S(1)}, u32[]{:S(2)}, u32[]{:S(2)}) %all-to-all-start) | async-done | bytes 1310752 | tf_op jit(solution)/shard_map/all_to_all | solution.py:160
  25.3 1.3 slice.34.q_ref
  26.6 13.9 %shard_map.97 = f32[512,1040]{1,0:T(8,128)} custom-call(bf16[512,1024]{1,0:T(8,128)(2,1)} %slice.34.q_ref, bf16[1024,128]{1,0:T(8,128)(2,1)} %k_ref.3, bf16[1024,128]{1,0:T(8,128)(2,1)} %v_ref.3), custom_call_target="tpu_custom_call" | custom-call | tf_op jit(solution)/shard_map/pallas_call | solution.py:148
  40.5 6.0 %all-to-all-start.1 = ((f32[16,32,1040]{2,1,0:T(8,128)}), f32[16,32,1040]{2,1,0:T(8,128)S(1)}, u32[]{:S(2)}, u32[]{:S(2)}) async-start(f32[16,32,1040]{2,1,0:T(8,128)} %bitcast.43), calls=%async_computation.1 | async-start | bytes 4718592 | tf_op jit(solution)/shard_map/all_to_all | solution.py:196
  46.5 0.9 broadcast_select_fusion
  47.4 1.3 collective-permute-start.1
  49.4 33.1 %collective-permute-done.1 = bf16[2,1024,128]{2,1,0:T(8,128)(2,1)} collective-permute-done((bf16[2,1024,128]{2,1,0:T(8,128)(2,1)}, bf16[2,1024,128]{2,1,0:T(8,128)(2,1)}, u32[]{:S(2)}, u32[]{:S(2)}) %collective-permute-start.1) | collective-permute-done | bytes 524320 | tf_op jit(solution)/shard_map/ppermute | solution.py:167
  82.5 1.9 broadcast_select_fusion.1
  84.4 1.3 collective-permute-start.2
  85.8 22.4 %copy.34 = bf16[8192,1024]{1,0:T(8,128)(2,1)} copy(bf16[8192,1024]{0,1:T(8,128)(2,1)} %bitcast.42) | data formatting | bytes 33554432 | tf_op jit(solution)/shard_map/dot_general | solution.py:224
  108.3 1.2 fusion.13
  110.3 1.1 broadcast_select_fusion.2
  111.4 2.1 %collective-permute-start.3 = (bf16[2,1024,128]{2,1,0:T(8,128)(2,1)S(1)}, bf16[2,1024,128]{2,1,0:T(8,128)(2,1)}, u32[]{:S(2)}, u32[]{:S(2)}) collective-permute-start(bf16[2,1024,128]{2,1,0:T(8,128)(2,1)S(1)} %broadcast_select_fusion.2), channel_id=1, source_target_pairs={{0,8},{16,24},{32,40},{48,56},{64,72},{80,88},{96,104},{112,120},{... | collective-permute-start | bytes 1572872 | tf_op jit(solution)/shard_map/ppermute | solution.py:167
  114.1 1.9 mul.45
  116.0 2.7 %mul.46 = f32[16,32,1024]{2,1,0:T(8,128)} reshape(f32[16,32,8,128]{3,2,1,0:T(8,128)} %mul.45) | data formatting | bytes 4194304 | tf_op jit(solution)/shard_map/mul | solution.py:222
  118.7 1.9 fusion
  120.6 1.2 fusion.5
  121.9 11.7 %fusion.14 = f32[32,8,1024]{2,0,1:T(8,128)} fusion(bf16[32,1024,1]{1,0,2:T(8,128)(2,1)S(1)} %reshape.117, bf16[8,1024,1024]{2,1,0:T(8,128)(2,1)} %bitcast.41), kind=kOutput, calls=%fused_computation.37 | convolution fusion | flops 536870912 | bytes 17891328 | tf_op jit(solution)/shard_map/dot_general | solution.py:224
  133.6 8.3 %all-to-all-start.2 = ((f32[32,8,1024]{2,0,1:T(8,128)}), f32[32,8,1024]{2,0,1:T(8,128)S(1)}, u32[]{:S(2)}, u32[]{:S(2)}) async-start(f32[32,8,1024]{2,0,1:T(8,128)} %fusion.14), calls=%async_computation.2 | async-start | bytes 2097152 | tf_op jit(solution)/shard_map/all_to_all | solution.py:226
  141.9 38.8 %shard_map.95.st_ref = f32[1024,1040]{1,0:T(8,128)} custom-call(bf16[1024,1024]{1,0:T(8,128)(2,1)} %q_ref.3, bf16[1024,128]{1,0:T(8,128)(2,1)} %k_ref.3, bf16[1024,128]{1,0:T(8,128)(2,1)} %v_ref.3), custom_call_target="tpu_custom_call" | custom-call | tf_op jit(solution)/shard_map/pallas_call | solution.py:64
  181.6 23.9 %shard_map.96 = f32[1024,1024]{1,0:T(8,128)} custom-call(s32[1]{0:T(128)} %bitcast.flag_ref, bf16[1024,1024]{1,0:T(8,128)(2,1)} %q_ref.3, bf16[1024,128]{1,0:T(8,128)(2,1)} %get-tuple-element.9.ka_ref, bf16[1024,128]{1,0:T(8,128)(2,1)} %get-tuple-element.8.va_ref, f32[1024,1040]{1,0:T(8,128)} %shard_map.95.st_ref), custom_call_target="tpu_custom_call" | custom-call | tf_op jit(solution)/shard_map/pallas_call | solution.py:119
  (40 shorter events, 4.8 us)
Async XLA Ops:
  0.6 7.7 %copy-start.2 = (bf16[1024,128]{1,0:T(8,128)(2,1)S(1)}, bf16[1024,128]{1,0:T(8,128)(2,1)}, u32[]{:S(2)}) copy-start(bf16[1024,128]{1,0:T(8,128)(2,1)} %k_ref.3) | copy-start | bytes 786436
  0.6 7.7 %copy-start = (bf16[1024,128]{1,0:T(8,128)(2,1)S(1)}, bf16[1024,128]{1,0:T(8,128)(2,1)}, u32[]{:S(2)}) copy-start(bf16[1024,128]{1,0:T(8,128)(2,1)} %v_ref.3) | copy-start | bytes 786436
  2.8 22.6 %all-to-all-start = ((bf16[16,32,1280]{2,1,0:T(8,128)(2,1)}), bf16[16,32,1280]{2,1,0:T(8,128)(2,1)S(1)}, u32[]{:S(2)}, u32[]{:S(2)}) async-start(bf16[16,32,1280]{2,1,0:T(8,128)(2,1)} %broadcast_in_dim.20), calls=%async_computation | async-start | bytes 2621440 | tf_op jit(solution)/shard_map/all_to_all | solution.py:160
  9.2 37.4 %collective-permute-start = (bf16[2,1024,128]{2,1,0:T(8,128)(2,1)}, bf16[2,1024,128]{2,1,0:T(8,128)(2,1)S(1)}, u32[]{:S(2)}, u32[]{:S(2)}) collective-permute-start(bf16[2,1024,128]{2,1,0:T(8,128)(2,1)} %pad_maximum_fusion), channel_id=1, source_target_pairs={{0,64},{1,65},{2,66},{3,67},{4,68},{5,69},{6,70},{7,71}} | collective-permute-start | bytes 1572872 | tf_op jit(solution)/shard_map/ppermute | solution.py:167
  25.3 15.1 %copy-start.4 = (bf16[16,32,1280]{2,1,0:T(8,128)(2,1)}, bf16[16,32,1280]{2,1,0:T(8,128)(2,1)S(1)}, u32[]{:S(2)}) copy-start(bf16[16,32,1280]{2,1,0:T(8,128)(2,1)S(1)} %all-to-all-done) | copy-start | bytes 3932164
  40.5 6.0 %copy-start.1 = (bf16[1024,128]{1,0:T(8,128)(2,1)S(1)}, bf16[1024,128]{1,0:T(8,128)(2,1)}, u32[]{:S(2)}) copy-start(bf16[1024,128]{1,0:T(8,128)(2,1)} %v_ref.3) | copy-start | bytes 786436
  40.5 6.0 %copy-start.3 = (bf16[1024,128]{1,0:T(8,128)(2,1)S(1)}, bf16[1024,128]{1,0:T(8,128)(2,1)}, u32[]{:S(2)}) copy-start(bf16[1024,128]{1,0:T(8,128)(2,1)} %k_ref.3) | copy-start | bytes 786436
  40.5 73.0 %all-to-all-start.1 = ((f32[16,32,1040]{2,1,0:T(8,128)}), f32[16,32,1040]{2,1,0:T(8,128)S(1)}, u32[]{:S(2)}, u32[]{:S(2)}) async-start(f32[16,32,1040]{2,1,0:T(8,128)} %bitcast.43), calls=%async_computation.1 | async-start | bytes 4718592 | tf_op jit(solution)/shard_map/all_to_all | solution.py:196
  47.4 35.0 %collective-permute-start.1 = (bf16[2,1024,128]{2,1,0:T(8,128)(2,1)}, bf16[2,1024,128]{2,1,0:T(8,128)(2,1)}, u32[]{:S(2)}, u32[]{:S(2)}) collective-permute-start(bf16[2,1024,128]{2,1,0:T(8,128)(2,1)} %broadcast_select_fusion), channel_id=1, source_target_pairs={{0,32},{64,96},{1,33},{65,97},{2,34},{66,98},{3,35},{67,99},{4,36}... | collective-permute-start | bytes 1572872 | tf_op jit(solution)/shard_map/ppermute | solution.py:167
  84.4 25.9 %collective-permute-start.2 = (bf16[2,1024,128]{2,1,0:T(8,128)(2,1)}, bf16[2,1024,128]{2,1,0:T(8,128)(2,1)S(1)}, u32[]{:S(2)}, u32[]{:S(2)}) collective-permute-start(bf16[2,1024,128]{2,1,0:T(8,128)(2,1)} %broadcast_select_fusion.1), channel_id=1, source_target_pairs={{0,16},{32,48},{64,80},{96,112},{1,17},{33,49},{65,81},{97,113},{2... | collective-permute-start | bytes 1572872 | tf_op jit(solution)/shard_map/ppermute | solution.py:167
  85.8 22.5 %copy-start.6 = (bf16[32,1024]{1,0:T(8,128)(2,1)S(1)}, bf16[32,1024]{1,0:T(8,128)(2,1)}, u32[]{:S(2)}) copy-start(bf16[32,1024]{1,0:T(8,128)(2,1)} %param.11) | copy-start | bytes 196612
  111.4 69.2 %collective-permute-start.3 = (bf16[2,1024,128]{2,1,0:T(8,128)(2,1)S(1)}, bf16[2,1024,128]{2,1,0:T(8,128)(2,1)}, u32[]{:S(2)}, u32[]{:S(2)}) collective-permute-start(bf16[2,1024,128]{2,1,0:T(8,128)(2,1)S(1)} %broadcast_select_fusion.2), channel_id=1, source_target_pairs={{0,8},{16,24},{32,40},{48,56},{64,72},{80,88},{96,104},{112,120},{... | collective-permute-start | bytes 1572872 | tf_op jit(solution)/shard_map/ppermute | solution.py:167
  118.7 1.9 copy-start.5
  133.6 71.9 %all-to-all-start.2 = ((f32[32,8,1024]{2,0,1:T(8,128)}), f32[32,8,1024]{2,0,1:T(8,128)S(1)}, u32[]{:S(2)}, u32[]{:S(2)}) async-start(f32[32,8,1024]{2,0,1:T(8,128)} %fusion.14), calls=%async_computation.2 | async-start | bytes 2097152 | tf_op jit(solution)/shard_map/all_to_all | solution.py:226

commit v4 on v2

--- a/solution.py
+++ b/solution.py
@@ -19,24 +19,43 @@
 
 def _ctx_kernel(flag_ref, q_ref, ka_ref, va_ref, ko_ref, vo_ref, o_ref):
     tq = q_ref.shape[0]
-    block = ko_ref.shape[0]
+    tiles = ko_ref.shape[0] // tq
     i = pl.program_id(1)
-    q = q_ref[...]
-    anchor_on = flag_ref[0] > 0
-    s_a = _dot_t(q, ka_ref[...]) * SCALE
-    s_o = _dot_t(q, ko_ref[...]) * SCALE
-    rows = i * tq + lax.broadcasted_iota(jnp.int32, (tq, block), 0)
-    cols = lax.broadcasted_iota(jnp.int32, (tq, block), 1)
-    own_vis = cols <= rows
-    s_a = jnp.where(anchor_on, s_a, NEGATIVE)
-    s_o = jnp.where(own_vis, s_o, NEGATIVE)
-    m = jnp.maximum(jnp.max(s_a, axis=1, keepdims=True), jnp.max(s_o, axis=1, keepdims=True))
-    w_a = jnp.where(anchor_on, jnp.exp(s_a - m), 0.0)
-    w_o = jnp.where(own_vis, jnp.exp(s_o - m), 0.0)
-    total = jnp.sum(w_a, axis=1, keepdims=True) + jnp.sum(w_o, axis=1, keepdims=True)
-    num = jnp.dot(w_a.astype(jnp.bfloat16), va_ref[...], preferred_element_type=jnp.float32)
-    num = num + jnp.dot(w_o.astype(jnp.bfloat16), vo_ref[...], preferred_element_type=jnp.float32)
-    o_ref[...] = num / total
+    rows = lax.broadcasted_iota(jnp.int32, (tq, tq), 0)
+    cols = lax.broadcasted_iota(jnp.int32, (tq, tq), 1)
+    diag_vis = cols <= rows
+
+    def tile(c, with_anchor):
+        q = q_ref[...]
+        parts = []
+        if with_anchor:
+            parts.append((_dot_t(q, ka_ref[...]) * SCALE, va_ref[...]))
+        if c > 0:
+            parts.append((_dot_t(q, ko_ref[:c * tq, :]) * SCALE, vo_ref[:c * tq, :]))
+        s_d = jnp.where(diag_vis, _dot_t(q, ko_ref[c * tq:(c + 1) * tq, :]) * SCALE, NEGATIVE)
+        parts.append((s_d, vo_ref[c * tq:(c + 1) * tq, :]))
+        m = parts[0][0].max(axis=1, keepdims=True)
+        for sc, _ in parts[1:]:
+            m = jnp.maximum(m, sc.max(axis=1, keepdims=True))
+        total = None
+        num = None
+        for sc, vals in parts:
+            p = jnp.exp(sc - m)
+            t = jnp.sum(p, axis=1, keepdims=True)
+            n = jnp.dot(p.astype(jnp.bfloat16), vals, preferred_element_type=jnp.float32)
+            total = t if total is None else total + t
+            num = n if num is None else num + n
+        o_ref[...] = num / total
+
+    on = flag_ref[0] > 0
+    for c in range(tiles):
+        @pl.when(jnp.logical_and(i == c, on))
+        def _(c=c):
+            tile(c, True)
+
+        @pl.when(jnp.logical_and(i == c, jnp.logical_not(on)))
+        def _(c=c):
+            tile(c, False)
 
 
 def ctx_attention(flag, q, ka, va, ko, vo, tq=256):
@@ -61,18 +80,39 @@
     )(flag, q, ka, va, ko, vo)
 
 
-def _part_kernel(q_ref, k_ref, v_ref, num_ref, m_ref, l_ref):
-    heads = q_ref.shape[1] // HEAD_WIDTH
+def _proj_kernel(a_ref, w_ref, o_ref):
+    o_ref[...] = jnp.dot(a_ref[...], w_ref[...], preferred_element_type=jnp.float32)
+
+
+def projection(a, w, tn=1024):
+    rows, inner = a.shape
+    cols = w.shape[1]
+    return pl.pallas_call(
+        _proj_kernel,
+        grid=(cols // tn,),
+        in_specs=[
+            pl.BlockSpec((rows, inner), lambda j: (0, 0)),
+            pl.BlockSpec((inner, tn), lambda j: (0, j)),
+        ],
+        out_specs=pl.BlockSpec((rows, tn), lambda j: (0, j)),
+        out_shape=jax.ShapeDtypeStruct((rows, cols), jnp.float32),
+        interpret=INTERPRET,
+    )(a, w)
+
+
+def _part_kernel(q_ref, k_ref, v_ref, st_ref):
+    width = q_ref.shape[1]
+    heads = width // HEAD_WIDTH
     k = k_ref[...]
     v = v_ref[...]
     for j in range(heads):
-        cols = slice(j * HEAD_WIDTH, (j + 1) * HEAD_WIDTH)
-        s = _dot_t(q_ref[:, cols], k) * SCALE
+        hc = slice(j * HEAD_WIDTH, (j + 1) * HEAD_WIDTH)
+        s = _dot_t(q_ref[:, hc], k) * SCALE
         m = jnp.max(s, axis=1, keepdims=True)
         w = jnp.exp(s - m)
-        m_ref[:, j:j + 1] = m
-        l_ref[:, j:j + 1] = jnp.sum(w, axis=1, keepdims=True)
-        num_ref[:, cols] = jnp.dot(w.astype(jnp.bfloat16), v, preferred_element_type=jnp.float32)
+        st_ref[:, width + j:width + j + 1] = m
+        st_ref[:, width + heads + j:width + heads + j + 1] = jnp.sum(w, axis=1, keepdims=True)
+        st_ref[:, hc] = jnp.dot(w.astype(jnp.bfloat16), v, preferred_element_type=jnp.float32)
 
 
 def part_attention(q, k, v, tq=128):
@@ -81,17 +121,12 @@
     heads = width // HEAD_WIDTH
     block = k.shape[0]
     kv_spec = pl.BlockSpec((block, HEAD_WIDTH), lambda i: (0, 0))
-    stat_spec = pl.BlockSpec((tq, heads), lambda i: (i, 0))
     return pl.pallas_call(
         _part_kernel,
         grid=(rows // tq,),
         in_specs=[pl.BlockSpec((tq, width), lambda i: (i, 0)), kv_spec, kv_spec],
-        out_specs=[pl.BlockSpec((tq, width), lambda i: (i, 0)), stat_spec, stat_spec],
-        out_shape=[
-            jax.ShapeDtypeStruct((rows, width), jnp.float32),
-            jax.ShapeDtypeStruct((rows, heads), jnp.float32),
-            jax.ShapeDtypeStruct((rows, heads), jnp.float32),
-        ],
+        out_specs=pl.BlockSpec((tq, width + 2 * heads), lambda i: (i, 0)),
+        out_shape=jax.ShapeDtypeStruct((rows, width + 2 * heads), jnp.float32),
         interpret=INTERPRET,
     )(q, k, v)
 
@@ -133,13 +168,12 @@
     all_k = gathered[:, width:width + HEAD_WIDTH]
     all_v = gathered[:, width + HEAD_WIDTH:]
 
-    num, mx, tot = part_attention(all_q, context_key_rows, context_value_rows)
-    state = jnp.concatenate([mx, tot, num], axis=1)
+    state = part_attention(all_q, context_key_rows, context_value_rows)
     state = lax.all_to_all(state, "ctx", 0, 0, tiled=True)
     state = state.reshape(n_ctx, resp_dev, -1)
-    m_s = state[:, :, :heads]
-    l_s = state[:, :, heads:2 * heads]
-    num_s = state[:, :, 2 * heads:].reshape(n_ctx, resp_dev, heads, HEAD_WIDTH)
+    num_s = state[:, :, :width].reshape(n_ctx, resp_dev, heads, HEAD_WIDTH)
+    m_s = state[:, :, width:width + heads]
+    l_s = state[:, :, width + heads:]
 
     own_rows = device * resp_dev + jnp.arange(resp_dev, dtype=jnp.int32)
     key_pos = jnp.arange(all_k.shape[0], dtype=jnp.int32)
@@ -163,10 +197,10 @@
     total = jnp.sum(l_s * f_s, axis=0) + l_r * f_r
     numer = jnp.sum(num_s * f_s[..., None], axis=0) + num_r * f_r[..., None]
     attended = (numer / total[..., None]).reshape(resp_dev, width).astype(jnp.bfloat16)
-    projected = jnp.dot(attended, out_weight, preferred_element_type=jnp.float32)
+    projected = projection(attended, out_weight)
     n_tp = lax.axis_size("tp")
-    projected = projected.reshape(resp_dev, n_tp, -1).transpose(1, 0, 2)
-    resp_out = jnp.sum(lax.all_to_all(projected, "tp", 0, 0), axis=0)
+    shares = lax.all_to_all(projected, "tp", 1, 0, tiled=True)
+    resp_out = jnp.sum(shares.reshape(n_tp, resp_dev, -1), axis=0)
 
     anchor = broadcast_from_first(
         jnp.stack([context_key_rows, context_value_rows]), "ctx", device, n_ctx

time: 195 us -> 166 us (0.85)
  local copies, waits for them, and re-layouts: 35.2 us -> 11.3 us
  matrix products: 14.1 us -> 2.4 us
  waiting for transfers between devices: 48.6 us -> 53.3 us
    dot_general x1 -> x0, local copies, waits for them, and re-layouts: 22.4 us -> none  [on_device(): jnp.dot(attended, out_weight, preferred_element_type=jnp.float32)]
    dot_general x1 -> x0, matrix products: 11.8 us -> none  [on_device(): jnp.dot(attended, out_weight, preferred_element_type=jnp.float32)]
    pallas_call x0 -> x1, Pallas kernels: none -> 10.2 us  [projection(): pl.pallas_call(_proj_kernel, grid=(cols // tn,), in_specs=[pl.BlockSpec((...]
    pallas_call x1, Pallas kernels: 45.8 us -> 36.4 us  [ctx_attention(): pl.pallas_call(_ctx_kernel, grid_spec=grid_spec, out_shape=jax.ShapeDtype...]
    ppermute x4, waiting for transfers between devices: 33.1 us -> 37.8 us  [broadcast_from_first(): got = lax.ppermute(x, axis, pairs)]
    concatenate x1 -> x0, local copies, waits for them, and re-layouts: 4.44 us -> none  [on_device(): state = jnp.concatenate([mx, tot, num], axis=1)]
    all_to_all x0 -> x1, local copies, waits for them, and re-layouts: none -> 2.3 us  [on_device(): shares = lax.all_to_all(projected, 'tp', 1, 0, tiled=True)]
  transfers between devices with their start and end apart: 7 -> 7, of which waited for: 2 -> 3; matrix products, arithmetic and copies ran while one was open for 29% -> 12% of each run, Pallas kernels for 31% -> 37%
where the time goes in v4:
time: 166 us; the launch traced here: 164 us
  Pallas kernels  60.5 us (36%)
  waiting for transfers between devices  53.3 us (32%)
  starting transfers between devices  25.2 us (15%)
  local copies, waits for them, and re-layouts  11.3 us (7%)
  other arithmetic  9.45 us (6%)
  matrix products  2.4 us (1%)
    ppermute x4, waiting for transfers between devices, broadcast_from_first(): got = lax.ppermute(x, axis, pairs)  37.8 us
    pallas_call x1, Pallas kernels, ctx_attention(): pl.pallas_call(_ctx_kernel, grid_spec=grid_spec, out_shape=jax.ShapeDtype...  36.4 us
    all_to_all x1, waiting for transfers between devices, gather_by_all_to_all(): lax.all_to_all(copies, axis, 0, 0).reshape((n * x.shape[0],) + x.shape[1:])  15.5 us
    pallas_call x1, Pallas kernels, part_attention(): pl.pallas_call(_part_kernel, grid=(rows // tq,), in_specs=[pl.BlockSpec((...  13.9 us
    pallas_call x1, Pallas kernels, projection(): pl.pallas_call(_proj_kernel, grid=(cols // tn,), in_specs=[pl.BlockSpec((...  10.2 us
    all_to_all x1, starting transfers between devices, on_device(): shares = lax.all_to_all(projected, 'tp', 1, 0, tiled=True)  8.27 us
    all_to_all x1, starting transfers between devices, on_device(): state = lax.all_to_all(state, 'ctx', 0, 0, tiled=True)  6.02 us
    all_to_all x1, starting transfers between devices, gather_by_all_to_all(): lax.all_to_all(copies, axis, 0, 0).reshape((n * x.shape[0],) + x.shape[1:])  5.51 us
  transfers between devices with their start and end apart: 7, of which 3 were waited for; matrix products, arithmetic and copies ran while one was open for 12% of the time, Pallas kernels for 37%

profile of v4, /device:TPU:22, one launch (start us, length us, event | category | flops | bytes accessed | tf_op | source)
XLA Modules:
  0.0 163.6 jit_solution(14315820631543634001)
XLA Ops:
  0.7 0.9 pad_maximum_fusion.1
  1.6 1.2 broadcast_in_dim.20
  2.8 5.5 %all-to-all-start = ((bf16[16,32,1280]{2,1,0:T(8,128)(2,1)}), bf16[16,32,1280]{2,1,0:T(8,128)(2,1)S(1)}, u32[]{:S(2)}, u32[]{:S(2)}) async-start(bf16[16,32,1280]{2,1,0:T(8,128)(2,1)} %broadcast_in_dim.20), calls=%async_computation | async-start | bytes 2621440 | tf_op jit(solution)/shard_map/all_to_all | solution.py:136
  9.9 15.5 %all-to-all-done = bf16[16,32,1280]{2,1,0:T(8,128)(2,1)S(1)} async-done(((bf16[16,32,1280]{2,1,0:T(8,128)(2,1)}), bf16[16,32,1280]{2,1,0:T(8,128)(2,1)S(1)}, u32[]{:S(2)}, u32[]{:S(2)}) %all-to-all-start) | async-done | bytes 1310752 | tf_op jit(solution)/shard_map/all_to_all | solution.py:136
  25.3 1.3 slice.34.q_ref
  26.6 13.9 %shard_map.96 = f32[512,1040]{1,0:T(8,128)} custom-call(bf16[512,1024]{1,0:T(8,128)(2,1)} %slice.34.q_ref, bf16[1024,128]{1,0:T(8,128)(2,1)} %k_ref.1, bf16[1024,128]{1,0:T(8,128)(2,1)} %v_ref.1), custom_call_target="tpu_custom_call" | custom-call | tf_op jit(solution)/shard_map/pallas_call | solution.py:124
  40.5 6.0 %all-to-all-start.1 = ((f32[16,32,1040]{2,1,0:T(8,128)}), f32[16,32,1040]{2,1,0:T(8,128)S(1)}, u32[]{:S(2)}, u32[]{:S(2)}) async-start(f32[16,32,1040]{2,1,0:T(8,128)} %bitcast.45), calls=%async_computation.1 | async-start | bytes 4718592 | tf_op jit(solution)/shard_map/all_to_all | solution.py:172
  46.6 0.9 broadcast_select_fusion
  47.4 1.3 collective-permute-start.1
  49.4 33.1 %collective-permute-done.1 = bf16[2,1024,128]{2,1,0:T(8,128)(2,1)} collective-permute-done((bf16[2,1024,128]{2,1,0:T(8,128)(2,1)}, bf16[2,1024,128]{2,1,0:T(8,128)(2,1)}, u32[]{:S(2)}, u32[]{:S(2)}) %collective-permute-start.1) | collective-permute-done | bytes 524320 | tf_op jit(solution)/shard_map/ppermute | solution.py:143
  82.5 1.9 %broadcast_select_fusion.1 = bf16[2,1024,128]{2,1,0:T(8,128)(2,1)} fusion(bf16[2,1024,128]{2,1,0:T(8,128)(2,1)} %collective-permute-done.1, pred[]{:T(512)S(6)} %eq.36, bf16[2,1024,128]{2,1,0:T(8,128)(2,1)S(1)} %collective-permute-done, bf16[1,1024,128]{2,1,0:T(8,128)(2,1)S(1)} %bitcast.48, bf16[1,1024,128]{2,1,0:T(8,128)(2,1)S(1)} %bitcast.51, pred[]{:T(512)S(6)} %eq.37), kind=kLoop, calls=%fused_computation.13 | loop fusion | flops 786432 | bytes 2097154 | tf_op jit(solution)/shard_map/jit(_where)/select_n | solution.py:144
  84.4 1.3 collective-permute-start.2
  85.8 1.2 fusion.13
  87.9 4.8 %collective-permute-done.2 = bf16[2,1024,128]{2,1,0:T(8,128)(2,1)S(1)} collective-permute-done((bf16[2,1024,128]{2,1,0:T(8,128)(2,1)}, bf16[2,1024,128]{2,1,0:T(8,128)(2,1)S(1)}, u32[]{:S(2)}, u32[]{:S(2)}) %collective-permute-start.2) | collective-permute-done | bytes 524320 | tf_op jit(solution)/shard_map/ppermute | solution.py:143
  92.7 1.1 broadcast_select_fusion.2
  93.8 2.1 %collective-permute-start.3 = (bf16[2,1024,128]{2,1,0:T(8,128)(2,1)S(1)}, bf16[2,1024,128]{2,1,0:T(8,128)(2,1)}, u32[]{:S(2)}, u32[]{:S(2)}) collective-permute-start(bf16[2,1024,128]{2,1,0:T(8,128)(2,1)S(1)} %broadcast_select_fusion.2), channel_id=1, source_target_pairs={{0,8},{16,24},{32,40},{48,56},{64,72},{80,88},{96,104},{112,120},{... | collective-permute-start | bytes 1572872 | tf_op jit(solution)/shard_map/ppermute | solution.py:143
  96.4 1.9 %mul.45 = f32[16,32,8,128]{3,2,1,0:T(8,128)} broadcast(f32[16,32,8]{2,1,0:T(8,128)S(1)} %get-tuple-element.5), dimensions={0,1,2} | broadcast | bytes 2113536 | tf_op jit(solution)/shard_map/mul | solution.py:198
  98.4 2.7 %mul.46 = f32[16,32,1024]{2,1,0:T(8,128)} reshape(f32[16,32,8,128]{3,2,1,0:T(8,128)} %mul.45) | data formatting | bytes 4194304 | tf_op jit(solution)/shard_map/mul | solution.py:198
  101.1 1.9 %fusion = f32[32,1024]{1,0:T(8,128)S(1)} fusion(f32[16,32,1024]{2,1,0:T(8,128)} %mul.46, f32[16,32,1040]{2,1,0:T(8,128)S(1)} %all-to-all-done.1), kind=kLoop, calls=%fused_computation.1 | loop fusion | flops 1015808 | bytes 4325376 | tf_op jit(solution)/shard_map/reduce_sum | solution.py:198
  103.0 1.2 fusion.5
  104.8 10.2 %shard_map.97 = f32[32,8192]{1,0:T(8,128)} custom-call(bf16[32,1024]{1,0:T(8,128)(2,1)} %bitcast.57, bf16[1024,8192]{1,0:T(8,128)(2,1)} %w_ref.1), custom_call_target="tpu_custom_call" | custom-call | tf_op jit(solution)/shard_map/pallas_call | solution.py:90
  115.0 2.3 %copy.47 = f32[4,8,8,1024]{3,2,0,1:T(8,128)} copy(f32[4,8,8,1024]{3,2,1,0:T(8,128)} %bitcast.55) | data formatting | bytes 2097152 | tf_op jit(solution)/shard_map/all_to_all | solution.py:202
  117.3 8.3 %all-to-all-start.2 = ((f32[32,8,1024]{2,0,1:T(8,128)}), f32[32,8,1024]{2,0,1:T(8,128)S(1)}, u32[]{:S(2)}, u32[]{:S(2)}) async-start(f32[32,8,1024]{2,0,1:T(8,128)} %bitcast.41), calls=%async_computation.2 | async-start | bytes 2097152 | tf_op jit(solution)/shard_map/all_to_all | solution.py:202
  126.5 36.4 %shard_map.95 = f32[1024,1024]{1,0:T(8,128)} custom-call(s32[1]{0:T(128)} %bitcast.flag_ref, bf16[1024,1024]{1,0:T(8,128)(2,1)} %q_ref.1, bf16[1024,128]{1,0:T(8,128)(2,1)} %get-tuple-element.9.ka_ref, bf16[1024,128]{1,0:T(8,128)(2,1)} %get-tuple-element.8.va_ref, bf16[1024,128]{1,0:T(8,128)(2,1)} %k_ref.1, bf16[1024,128]{1,0:T(8,128)(2,1)} %v_ref.1), custom_call_target="tpu_custom_call" | custom-call | tf_op jit(solution)/shard_map/pallas_call | solution.py:75
  (39 shorter events, 5.4 us)
Async XLA Ops:
  0.6 7.7 %copy-start.2 = (bf16[1024,128]{1,0:T(8,128)(2,1)S(1)}, bf16[1024,128]{1,0:T(8,128)(2,1)}, u32[]{:S(2)}) copy-start(bf16[1024,128]{1,0:T(8,128)(2,1)} %k_ref.1) | copy-start | bytes 786436
  0.6 7.7 %copy-start = (bf16[1024,128]{1,0:T(8,128)(2,1)S(1)}, bf16[1024,128]{1,0:T(8,128)(2,1)}, u32[]{:S(2)}) copy-start(bf16[1024,128]{1,0:T(8,128)(2,1)} %v_ref.1) | copy-start | bytes 786436
  2.8 22.6 %all-to-all-start = ((bf16[16,32,1280]{2,1,0:T(8,128)(2,1)}), bf16[16,32,1280]{2,1,0:T(8,128)(2,1)S(1)}, u32[]{:S(2)}, u32[]{:S(2)}) async-start(bf16[16,32,1280]{2,1,0:T(8,128)(2,1)} %broadcast_in_dim.20), calls=%async_computation | async-start | bytes 2621440 | tf_op jit(solution)/shard_map/all_to_all | solution.py:136
  9.2 37.4 %collective-permute-start = (bf16[2,1024,128]{2,1,0:T(8,128)(2,1)}, bf16[2,1024,128]{2,1,0:T(8,128)(2,1)S(1)}, u32[]{:S(2)}, u32[]{:S(2)}) collective-permute-start(bf16[2,1024,128]{2,1,0:T(8,128)(2,1)} %pad_maximum_fusion), channel_id=1, source_target_pairs={{0,64},{1,65},{2,66},{3,67},{4,68},{5,69},{6,70},{7,71}} | collective-permute-start | bytes 1572872 | tf_op jit(solution)/shard_map/ppermute | solution.py:143
  25.3 15.2 %copy-start.4 = (bf16[16,32,1280]{2,1,0:T(8,128)(2,1)}, bf16[16,32,1280]{2,1,0:T(8,128)(2,1)S(1)}, u32[]{:S(2)}) copy-start(bf16[16,32,1280]{2,1,0:T(8,128)(2,1)S(1)} %all-to-all-done) | copy-start | bytes 3932164
  40.5 6.0 %copy-start.1 = (bf16[1024,128]{1,0:T(8,128)(2,1)S(1)}, bf16[1024,128]{1,0:T(8,128)(2,1)}, u32[]{:S(2)}) copy-start(bf16[1024,128]{1,0:T(8,128)(2,1)} %v_ref.1) | copy-start | bytes 786436
  40.5 6.1 %copy-start.3 = (bf16[1024,128]{1,0:T(8,128)(2,1)S(1)}, bf16[1024,128]{1,0:T(8,128)(2,1)}, u32[]{:S(2)}) copy-start(bf16[1024,128]{1,0:T(8,128)(2,1)} %k_ref.1) | copy-start | bytes 786436
  40.5 55.4 %all-to-all-start.1 = ((f32[16,32,1040]{2,1,0:T(8,128)}), f32[16,32,1040]{2,1,0:T(8,128)S(1)}, u32[]{:S(2)}, u32[]{:S(2)}) async-start(f32[16,32,1040]{2,1,0:T(8,128)} %bitcast.45), calls=%async_computation.1 | async-start | bytes 4718592 | tf_op jit(solution)/shard_map/all_to_all | solution.py:172
  46.5 39.3 %copy-start.6 = (bf16[32,1024]{1,0:T(8,128)(2,1)S(1)}, bf16[32,1024]{1,0:T(8,128)(2,1)}, u32[]{:S(2)}) copy-start(bf16[32,1024]{1,0:T(8,128)(2,1)} %param.11) | copy-start | bytes 196612
  47.4 35.1 %collective-permute-start.1 = (bf16[2,1024,128]{2,1,0:T(8,128)(2,1)}, bf16[2,1024,128]{2,1,0:T(8,128)(2,1)}, u32[]{:S(2)}, u32[]{:S(2)}) collective-permute-start(bf16[2,1024,128]{2,1,0:T(8,128)(2,1)} %broadcast_select_fusion), channel_id=1, source_target_pairs={{0,32},{64,96},{1,33},{65,97},{2,34},{66,98},{3,35},{67,99},{4,36}... | collective-permute-start | bytes 1572872 | tf_op jit(solution)/shard_map/ppermute | solution.py:143
  84.4 8.3 %collective-permute-start.2 = (bf16[2,1024,128]{2,1,0:T(8,128)(2,1)}, bf16[2,1024,128]{2,1,0:T(8,128)(2,1)S(1)}, u32[]{:S(2)}, u32[]{:S(2)}) collective-permute-start(bf16[2,1024,128]{2,1,0:T(8,128)(2,1)} %broadcast_select_fusion.1), channel_id=1, source_target_pairs={{0,16},{32,48},{64,80},{96,112},{1,17},{33,49},{65,81},{97,113},{2... | collective-permute-start | bytes 1572872 | tf_op jit(solution)/shard_map/ppermute | solution.py:143
  93.8 31.8 %collective-permute-start.3 = (bf16[2,1024,128]{2,1,0:T(8,128)(2,1)S(1)}, bf16[2,1024,128]{2,1,0:T(8,128)(2,1)}, u32[]{:S(2)}, u32[]{:S(2)}) collective-permute-start(bf16[2,1024,128]{2,1,0:T(8,128)(2,1)S(1)} %broadcast_select_fusion.2), channel_id=1, source_target_pairs={{0,8},{16,24},{32,40},{48,56},{64,72},{80,88},{96,104},{112,120},{... | collective-permute-start | bytes 1572872 | tf_op jit(solution)/shard_map/ppermute | solution.py:143
  101.1 1.9 %copy-start.5 = (bf16[32,8,512]{2,0,1:T(8,128)(2,1)S(1)}, bf16[32,8,512]{2,0,1:T(8,128)(2,1)}, u32[]{:S(2)}) copy-start(bf16[32,8,512]{2,0,1:T(8,128)(2,1)} %get-tuple-element.7) | copy-start | bytes 786436
  117.3 45.6 %all-to-all-start.2 = ((f32[32,8,1024]{2,0,1:T(8,128)}), f32[32,8,1024]{2,0,1:T(8,128)S(1)}, u32[]{:S(2)}, u32[]{:S(2)}) async-start(f32[32,8,1024]{2,0,1:T(8,128)} %bitcast.41), calls=%async_computation.2 | async-start | bytes 2097152 | tf_op jit(solution)/shard_map/all_to_all | solution.py:202

commit v5 on v4

--- a/solution.py
+++ b/solution.py
@@ -80,24 +80,44 @@
     )(flag, q, ka, va, ko, vo)
 
 
-def _proj_kernel(a_ref, w_ref, o_ref):
-    o_ref[...] = jnp.dot(a_ref[...], w_ref[...], preferred_element_type=jnp.float32)
-
-
-def projection(a, w, tn=1024):
-    rows, inner = a.shape
-    cols = w.shape[1]
+def _finish_kernel(st_ref, own_ref, w_ref, o_ref, att_ref):
+    width = att_ref.shape[1]
+    heads = width // HEAD_WIDTH
+
+    @pl.when(pl.program_id(0) == 0)
+    def _():
+        for h in range(heads):
+            hc = slice(h * HEAD_WIDTH, (h + 1) * HEAD_WIDTH)
+            mc = slice(width + h, width + h + 1)
+            lc = slice(width + heads + h, width + heads + h + 1)
+            m_s = st_ref[:, :, mc]
+            m_r = own_ref[:, mc]
+            top = jnp.maximum(jnp.max(m_s, axis=0), m_r)
+            f_s = jnp.exp(m_s - top[None])
+            f_r = jnp.exp(m_r - top)
+            total = jnp.sum(st_ref[:, :, lc] * f_s, axis=0) + own_ref[:, lc] * f_r
+            numer = jnp.sum(st_ref[:, :, hc] * f_s, axis=0) + own_ref[:, hc] * f_r
+            att_ref[:, hc] = (numer / total).astype(att_ref.dtype)
+
+    o_ref[...] = jnp.dot(att_ref[...], w_ref[...], preferred_element_type=jnp.float32)
+
+
+def finish_projection(state, own, w, tn=1024):
+    sources, rows, packed = state.shape
+    inner, cols = w.shape
     return pl.pallas_call(
-        _proj_kernel,
+        _finish_kernel,
         grid=(cols // tn,),
         in_specs=[
-            pl.BlockSpec((rows, inner), lambda j: (0, 0)),
+            pl.BlockSpec((sources, rows, packed), lambda j: (0, 0, 0)),
+            pl.BlockSpec((rows, packed), lambda j: (0, 0)),
             pl.BlockSpec((inner, tn), lambda j: (0, j)),
         ],
         out_specs=pl.BlockSpec((rows, tn), lambda j: (0, j)),
         out_shape=jax.ShapeDtypeStruct((rows, cols), jnp.float32),
+        scratch_shapes=[pltpu.VMEM((rows, inner), jnp.bfloat16)],
         interpret=INTERPRET,
-    )(a, w)
+    )(state, own, w)
 
 
 def _part_kernel(q_ref, k_ref, v_ref, st_ref):
@@ -169,11 +189,19 @@
     all_v = gathered[:, width + HEAD_WIDTH:]
 
     state = part_attention(all_q, context_key_rows, context_value_rows)
+
+    anchor = broadcast_from_first(
+        jnp.stack([context_key_rows, context_value_rows]), "ctx", device, n_ctx
+    )
+    anchor, state = lax.optimization_barrier((anchor, state))
     state = lax.all_to_all(state, "ctx", 0, 0, tiled=True)
+
+    flag = (device > 0).astype(jnp.int32).reshape(1)
+    ctx_out = ctx_attention(
+        flag, ctx_queries, anchor[0], anchor[1], context_key_rows, context_value_rows
+    )
+    ctx_out, state = lax.optimization_barrier((ctx_out, state))
     state = state.reshape(n_ctx, resp_dev, -1)
-    num_s = state[:, :, :width].reshape(n_ctx, resp_dev, heads, HEAD_WIDTH)
-    m_s = state[:, :, width:width + heads]
-    l_s = state[:, :, width + heads:]
 
     own_rows = device * resp_dev + jnp.arange(resp_dev, dtype=jnp.int32)
     key_pos = jnp.arange(all_k.shape[0], dtype=jnp.int32)
@@ -190,25 +218,11 @@
     num_r = jnp.einsum(
         "rhk,kd->rhd", w_r.astype(jnp.bfloat16), all_v, preferred_element_type=jnp.float32
     )
-
-    top = jnp.maximum(jnp.max(m_s, axis=0), m_r)
-    f_s = jnp.exp(m_s - top[None])
-    f_r = jnp.exp(m_r - top)
-    total = jnp.sum(l_s * f_s, axis=0) + l_r * f_r
-    numer = jnp.sum(num_s * f_s[..., None], axis=0) + num_r * f_r[..., None]
-    attended = (numer / total[..., None]).reshape(resp_dev, width).astype(jnp.bfloat16)
-    projected = projection(attended, out_weight)
+    own = jnp.concatenate([num_r.reshape(resp_dev, width), m_r, l_r], axis=1)
+    projected = finish_projection(state, own, out_weight)
     n_tp = lax.axis_size("tp")
     shares = lax.all_to_all(projected, "tp", 1, 0, tiled=True)
     resp_out = jnp.sum(shares.reshape(n_tp, resp_dev, -1), axis=0)
-
-    anchor = broadcast_from_first(
-        jnp.stack([context_key_rows, context_value_rows]), "ctx", device, n_ctx
-    )
-    flag = (device > 0).astype(jnp.int32).reshape(1)
-    ctx_out = ctx_attention(
-        flag, ctx_queries, anchor[0], anchor[1], context_key_rows, context_value_rows
-    )
     return (ctx_out, resp_out)
 
 

time: 166 us -> 157 us (0.946)
  the two profiles are of different devices: /device:TPU:22 before, /device:TPU:4 now
where the time goes in v5:
time: 157 us; the launch traced here: 155 us
  Pallas kernels  62.6 us (40%)
  waiting for transfers between devices  32.8 us (21%)
  blocking collectives  25.2 us (16%)
  starting transfers between devices  17.8 us (11%)
  local copies, waits for them, and re-layouts  6.91 us (4%)
  other arithmetic  4.54 us (3%)
  matrix products  3.1 us (2%)
    pallas_call x1, Pallas kernels, ctx_attention(): pl.pallas_call(_ctx_kernel, grid_spec=grid_spec, out_shape=jax.ShapeDtype...  36.4 us
    all_to_all x1, blocking collectives, on_device(): shares = lax.all_to_all(projected, 'tp', 1, 0, tiled=True)  25.2 us
    ppermute x4, waiting for transfers between devices, broadcast_from_first(): got = lax.ppermute(x, axis, pairs)  17.9 us
    all_to_all x1, waiting for transfers between devices, gather_by_all_to_all(): lax.all_to_all(copies, axis, 0, 0).reshape((n * x.shape[0],) + x.shape[1:])  14.9 us
    pallas_call x1, Pallas kernels, part_attention(): pl.pallas_call(_part_kernel, grid=(rows // tq,), in_specs=[pl.BlockSpec((...  13.9 us
    pallas_call x1, Pallas kernels, finish_projection(): pl.pallas_call(_finish_kernel, grid=(cols // tn,), in_specs=[pl.BlockSpec...  12.3 us
    ppermute x4, starting transfers between devices, broadcast_from_first(): got = lax.ppermute(x, axis, pairs)  6.12 us
    all_to_all x1, starting transfers between devices, on_device(): state = lax.all_to_all(state, 'ctx', 0, 0, tiled=True)  5.86 us
  transfers between devices with their start and end apart: 6, of which 3 were waited for; matrix products, arithmetic and copies ran while one was open for 6% of the time, Pallas kernels for 33%

profile of v5, /device:TPU:4, one launch (start us, length us, event | category | flops | bytes accessed | tf_op | source)
XLA Modules:
  0.0 154.5 jit_solution(7357208848282968145)
XLA Ops:
  0.7 1.1 pad_maximum_fusion
  1.8 1.3 collective-permute-start
  3.1 11.3 %collective-permute-done = bf16[2,1024,128]{2,1,0:T(8,128)(2,1)S(1)} collective-permute-done((bf16[2,1024,128]{2,1,0:T(8,128)(2,1)S(1)}, bf16[2,1024,128]{2,1,0:T(8,128)(2,1)S(1)}, u32[]{:S(2)}, u32[]{:S(2)}) %collective-permute-start) | collective-permute-done | bytes 524320 | tf_op jit(solution)/shard_map/ppermute | solution.py:163
  14.4 1.1 broadcast_select_fusion
  15.5 1.5 collective-permute-start.1
  17.0 6.6 %collective-permute-done.1 = bf16[2,1024,128]{2,1,0:T(8,128)(2,1)S(1)} collective-permute-done((bf16[2,1024,128]{2,1,0:T(8,128)(2,1)S(1)}, bf16[2,1024,128]{2,1,0:T(8,128)(2,1)S(1)}, u32[]{:S(2)}, u32[]{:S(2)}) %collective-permute-start.1) | collective-permute-done | bytes 524320 | tf_op jit(solution)/shard_map/ppermute | solution.py:163
  23.7 1.3 collective-permute-start.2
  25.1 1.2 broadcast_in_dim.31
  26.3 5.8 %all-to-all-start = ((bf16[16,32,1280]{2,1,0:T(8,128)(2,1)}), bf16[16,32,1280]{2,1,0:T(8,128)(2,1)S(1)}, u32[]{:S(2)}, u32[]{:S(2)}) async-start(bf16[16,32,1280]{2,1,0:T(8,128)(2,1)} %broadcast_in_dim.31), calls=%async_computation | async-start | bytes 2621440 | tf_op jit(solution)/shard_map/all_to_all | solution.py:156
  32.2 2.1 %collective-permute-start.3 = (bf16[2,1024,128]{2,1,0:T(8,128)(2,1)S(1)}, bf16[2,1024,128]{2,1,0:T(8,128)(2,1)S(1)}, u32[]{:S(2)}, u32[]{:S(2)}) collective-permute-start(bf16[2,1024,128]{2,1,0:T(8,128)(2,1)S(1)} %broadcast_select_fusion.2), channel_id=1, source_target_pairs={{0,8},{16,24},{32,40},{48,56},{64,72},{80,88},{96,104},{112,120},{... | collective-permute-start | bytes 1572872 | tf_op jit(solution)/shard_map/ppermute | solution.py:163
  34.3 14.9 %all-to-all-done = bf16[16,32,1280]{2,1,0:T(8,128)(2,1)S(1)} async-done(((bf16[16,32,1280]{2,1,0:T(8,128)(2,1)}), bf16[16,32,1280]{2,1,0:T(8,128)(2,1)S(1)}, u32[]{:S(2)}, u32[]{:S(2)}) %all-to-all-start) | async-done | bytes 1310752 | tf_op jit(solution)/shard_map/all_to_all | solution.py:156
  49.2 1.2 slice.20.q_ref
  50.4 13.9 %shard_map.95 = f32[512,1040]{1,0:T(8,128)} custom-call(bf16[512,1024]{1,0:T(8,128)(2,1)} %slice.20.q_ref, bf16[1024,128]{1,0:T(8,128)(2,1)} %ko_ref.1, bf16[1024,128]{1,0:T(8,128)(2,1)} %vo_ref.1), custom_call_target="tpu_custom_call" | custom-call | tf_op jit(solution)/shard_map/pallas_call | solution.py:144
  64.3 5.9 %all-to-all-start.1 = ((f32[16,32,1040]{2,1,0:T(8,128)}), f32[16,32,1040]{2,1,0:T(8,128)S(1)}, u32[]{:S(2)}, u32[]{:S(2)}) async-start(f32[16,32,1040]{2,1,0:T(8,128)} %bitcast.43), calls=%async_computation.1 | async-start | bytes 4718592 | tf_op jit(solution)/shard_map/all_to_all | solution.py:197
  71.0 1.9 %fusion.9 = (f32[32,8]{0,1:T(8,128)S(1)}, f32[32,8,512]{2,0,1:T(8,128)}) fusion(bf16[512,1280]{1,0:T(8,128)(2,1)} %bitcast.51, pred[32,512]{1,0:T(8,128)(4,1)S(1)} %fusion.8, bf16[32,1024]{1,0:T(8,128)(2,1)S(1)} %copy-done.4), kind=kOutput, calls=%fused_computation.27 | convolution fusion | flops 33947392 | bytes 738304 | tf_op jit(solution)/shard_map/rhd,kd->rhk/dot_general | solution.py:213
  73.0 1.3 fusion.2
  74.4 1.2 fusion.4
  75.6 0.7 concatenate.7.own_ref
  76.3 0.8 slice_bitcast_fusion
  77.1 36.4 %shard_map.96 = f32[1024,1024]{1,0:T(8,128)} custom-call(s32[1]{0:T(128)} %bitcast.flag_ref, bf16[1024,1024]{1,0:T(8,128)(2,1)} %q_ref.1, bf16[1024,128]{1,0:T(8,128)(2,1)} %get-tuple-element.13.ka_ref, bf16[1024,128]{1,0:T(8,128)(2,1)} %get-tuple-element.12.va_ref, bf16[1024,128]{1,0:T(8,128)(2,1)} %ko_ref.1, bf16[1024,128]{1,0:T(8,128)(2,1)} %vo_ref.1), custom_call_target="tpu_custom_call" | custom-call | tf_op jit(solution)/shard_map/pallas_call | solution.py:75
  113.5 1.4 copy-done
  114.9 12.3 %shard_map.97 = f32[32,8192]{1,0:T(8,128)} custom-call(f32[16,32,1040]{2,1,0:T(8,128)} %copy-done, f32[32,1040]{1,0:T(8,128)} %concatenate.7.own_ref, bf16[1024,8192]{1,0:T(8,128)(2,1)} %w_ref.1), custom_call_target="tpu_custom_call" | custom-call | tf_op jit(solution)/shard_map/pallas_call | solution.py:108
  127.3 1.3 copy.31
  128.6 25.2 %all_to_all.30 = f32[32,8,1024]{2,0,1:T(8,128)S(1)} all-to-all(f32[32,8,1024]{2,0,1:T(8,128)S(1)} %bitcast.54), channel_id=1, replica_groups=mesh['ctx'=16,'tp'=8] {'tp'}, dimensions={1} | all-to-all | bytes 2097152 | tf_op jit(solution)/shard_map/all_to_all | solution.py:224
  (28 shorter events, 1.2 us)
Async XLA Ops:
  0.6 23.0 %copy-start.1 = (bf16[1024,128]{1,0:T(8,128)(2,1)S(1)}, bf16[1024,128]{1,0:T(8,128)(2,1)}, u32[]{:S(2)}) copy-start(bf16[1024,128]{1,0:T(8,128)(2,1)} %vo_ref.1) | copy-start | bytes 786436
  0.6 23.0 %copy-start.2 = (bf16[1024,128]{1,0:T(8,128)(2,1)S(1)}, bf16[1024,128]{1,0:T(8,128)(2,1)}, u32[]{:S(2)}) copy-start(bf16[1024,128]{1,0:T(8,128)(2,1)} %ko_ref.1) | copy-start | bytes 786436
  1.8 12.6 %collective-permute-start = (bf16[2,1024,128]{2,1,0:T(8,128)(2,1)S(1)}, bf16[2,1024,128]{2,1,0:T(8,128)(2,1)S(1)}, u32[]{:S(2)}, u32[]{:S(2)}) collective-permute-start(bf16[2,1024,128]{2,1,0:T(8,128)(2,1)S(1)} %pad_maximum_fusion), channel_id=1, source_target_pairs={{0,64},{1,65},{2,66},{3,67},{4,68},{5,69},{6,70},{7,71}} | collective-permute-start | bytes 1572872 | tf_op jit(solution)/shard_map/ppermute | solution.py:163
  15.5 9.6 %copy-start.4 = (bf16[32,1024]{1,0:T(8,128)(2,1)S(1)}, bf16[32,1024]{1,0:T(8,128)(2,1)}, u32[]{:S(2)}) copy-start(bf16[32,1024]{1,0:T(8,128)(2,1)} %param.11) | copy-start | bytes 196612
  15.5 9.6 %copy-start.5 = (bf16[32,128]{1,0:T(8,128)(2,1)S(1)}, bf16[32,128]{1,0:T(8,128)(2,1)}, u32[]{:S(2)}) copy-start(bf16[32,128]{1,0:T(8,128)(2,1)} %param.13) | copy-start | bytes 24580
  15.5 9.6 %copy-start.6 = (bf16[32,128]{1,0:T(8,128)(2,1)S(1)}, bf16[32,128]{1,0:T(8,128)(2,1)}, u32[]{:S(2)}) copy-start(bf16[32,128]{1,0:T(8,128)(2,1)} %param.12) | copy-start | bytes 24580
  15.5 8.1 %collective-permute-start.1 = (bf16[2,1024,128]{2,1,0:T(8,128)(2,1)S(1)}, bf16[2,1024,128]{2,1,0:T(8,128)(2,1)S(1)}, u32[]{:S(2)}, u32[]{:S(2)}) collective-permute-start(bf16[2,1024,128]{2,1,0:T(8,128)(2,1)S(1)} %broadcast_select_fusion), channel_id=1, source_target_pairs={{0,32},{64,96},{1,33},{65,97},{2,34},{66,98},{3,35},{67,99},{4,36}... | collective-permute-start | bytes 1572872 | tf_op jit(solution)/shard_map/ppermute | solution.py:163
  23.7 8.4 %collective-permute-start.2 = (bf16[2,1024,128]{2,1,0:T(8,128)(2,1)S(1)}, bf16[2,1024,128]{2,1,0:T(8,128)(2,1)S(1)}, u32[]{:S(2)}, u32[]{:S(2)}) collective-permute-start(bf16[2,1024,128]{2,1,0:T(8,128)(2,1)S(1)} %broadcast_select_fusion.1), channel_id=1, source_target_pairs={{0,16},{32,48},{64,80},{96,112},{1,17},{33,49},{65,81},{97,113},{2... | collective-permute-start | bytes 1572872 | tf_op jit(solution)/shard_map/ppermute | solution.py:163
  26.3 22.9 %all-to-all-start = ((bf16[16,32,1280]{2,1,0:T(8,128)(2,1)}), bf16[16,32,1280]{2,1,0:T(8,128)(2,1)S(1)}, u32[]{:S(2)}, u32[]{:S(2)}) async-start(bf16[16,32,1280]{2,1,0:T(8,128)(2,1)} %broadcast_in_dim.31), calls=%async_computation | async-start | bytes 2621440 | tf_op jit(solution)/shard_map/all_to_all | solution.py:156
  32.2 32.1 %collective-permute-start.3 = (bf16[2,1024,128]{2,1,0:T(8,128)(2,1)S(1)}, bf16[2,1024,128]{2,1,0:T(8,128)(2,1)S(1)}, u32[]{:S(2)}, u32[]{:S(2)}) collective-permute-start(bf16[2,1024,128]{2,1,0:T(8,128)(2,1)S(1)} %broadcast_select_fusion.2), channel_id=1, source_target_pairs={{0,8},{16,24},{32,40},{48,56},{64,72},{80,88},{96,104},{112,120},{... | collective-permute-start | bytes 1572872 | tf_op jit(solution)/shard_map/ppermute | solution.py:163
  49.2 15.1 %copy-start.3 = (bf16[16,32,1280]{2,1,0:T(8,128)(2,1)}, bf16[16,32,1280]{2,1,0:T(8,128)(2,1)S(1)}, u32[]{:S(2)}) copy-start(bf16[16,32,1280]{2,1,0:T(8,128)(2,1)S(1)} %all-to-all-done) | copy-start | bytes 3932164
  64.3 49.2 %all-to-all-start.1 = ((f32[16,32,1040]{2,1,0:T(8,128)}), f32[16,32,1040]{2,1,0:T(8,128)S(1)}, u32[]{:S(2)}, u32[]{:S(2)}) async-start(f32[16,32,1040]{2,1,0:T(8,128)} %bitcast.43), calls=%async_computation.1 | async-start | bytes 4718592 | tf_op jit(solution)/shard_map/all_to_all | solution.py:197
  113.5 1.4 copy-start
